TPU v7x, 512 devices: a whole 4x8x8 slice. The times are simulated.
512 devices in a mesh: space: 32 (over y, x_lo, core), modes: 16 (over z, x_hi).
Axes of the slice: x: 4 (x_hi: 2, x_lo: 2; x = x_hi * 2 + x_lo), y: 8, z: 8, core: 2. Of those that a mesh axis runs over, the one named last changes fastest.
Arguments:
- rhs: bfloat16 [2, 256, 512, 512], P(None, 'modes', 'space'), may hold values from -6 to 6
- initial: bfloat16 [2, 256, 512, 512], P(None, 'modes', 'space'), may hold values from -6 to 6
- region: int32 [512, 512], P('space'), may hold values from 0 to 7
- base_table: float32 [2, 8], replicated, may hold values from 0.5 to 4
- term_table: float32 [2, 3, 8], replicated, may hold values from -0.3 to 0.3
- galerkin: bfloat16 [3, 256, 256], replicated, may hold values from -0.375 to 0.375
- block_mask: int32 [3, 16, 16], replicated, may hold values from 0 to 1, as said below
- block_inverse: float32 [16, 16, 16], P('modes'), as said below
Outputs:
- solution: float32 [2, 256, 512, 512], P(None, 'modes', 'space')
Inputs may be any that keep to these rules, and one draw needn't show every extreme that they name: `block_mask`: each mode block is coupled with itself by every term, and some pairs of mode blocks are not coupled. `block_inverse`: blocks near the identity, off-diagonal entries at most 0.3 in magnitude.
All inputs are finite; a program needn't handle non-finite values.
Results may differ from a plain program's by a relative error of at most 0.0017.
Values may be sent and summed in bfloat16 or wider, within the bound.
No kernel may reach another device: no remote copies, remote signals or barrier semaphores. Data moves between devices by JAX's collectives and lax.ppermute only.
A program may use at most 64 MiB of HBM per device.

v0:
```python
import jax
import jax.numpy as jnp
from jax import lax
from jax.sharding import PartitionSpec as P

SWEEPS = 2


def with_halo(block, sides, width):
    for axis, dim in sides:
        count = lax.axis_size(axis)
        forward = [(i, i + 1) for i in range(count - 1)]
        forward.append((count - 1, 0))
        backward = [(target, source) for source, target in forward]
        low = lax.ppermute(
            lax.slice_in_dim(block, block.shape[dim] - width, None, axis=dim), axis, forward
        )
        high = lax.ppermute(lax.slice_in_dim(block, 0, width, axis=dim), axis, backward)
        block = jnp.concatenate([low, block, high], axis=dim)
    return block


def lookup(table, region):
    total = jnp.zeros(table.shape[:-1] + region.shape, jnp.float32)
    for which in range(table.shape[-1]):
        total = total + table[..., which, None, None] * (region == which).astype(jnp.float32)
    return total


def laplace_padded(padded):
    center = padded[..., 1:-1, :]
    zeros = jnp.zeros(center.shape[:-1] + (1,), jnp.float32)
    right = jnp.concatenate([center[..., 1:], zeros], -1)
    left = jnp.concatenate([zeros, center[..., :-1]], -1)
    return 4.0 * center - padded[..., 2:, :] - padded[..., :-2, :] - right - left


def body(rhs, initial, region, base_table, term_table, galerkin, block_mask, block_inverse):
    terms = galerkin.shape[0]
    modes_all = galerkin.shape[1]
    blocks = block_mask.shape[1]
    width = modes_all // blocks
    shaped = galerkin.reshape(terms, blocks, width, blocks, width)
    coupling = (shaped * block_mask[:, :, None, :, None].astype(jnp.bfloat16)).reshape(
        terms, modes_all, modes_all
    )
    base = lookup(base_table, region)
    coef = lookup(term_table, region)
    rhs_float = rhs.astype(jnp.float32)
    inverse_base = 1.0 / (4.0 * base[:, None])
    u_field = initial.astype(jnp.float32)
    for sweep in range(SWEEPS):
        padded = with_halo(u_field, (("space", 2),), 1)
        local = base[:, None] * laplace_padded(padded)
        rounded = lax.optimization_barrier(padded.astype(jnp.bfloat16)).astype(jnp.float32)
        lap_rounded = laplace_padded(rounded)
        tiles = (coef[:, :, None] * lap_rounded[:, None]).astype(jnp.bfloat16)
        mix_tiles = lax.all_to_all(tiles, "modes", split_axis=3, concat_axis=2, tiled=True)
        coupled = lax.all_to_all(
            jnp.einsum(
                "kij,fkjxy->fixy", coupling, mix_tiles, preferred_element_type=jnp.float32
            ).astype(jnp.bfloat16),
            "modes",
            split_axis=1,
            concat_axis=2,
            tiled=True,
        )
        resid = rhs_float - local - coupled.astype(jnp.float32)
        scaled = resid * inverse_base
        fields, modes_dev, cells_x, cells_y = scaled.shape
        grouped = scaled.reshape(fields, modes_dev // width, width, cells_x, cells_y)
        update = jnp.einsum(
            "bac,fbcxy->fbaxy", block_inverse, grouped, precision=lax.Precision.HIGHEST
        )
        u_field = u_field + 0.6 * update.reshape(fields, modes_dev, cells_x, cells_y)
    return u_field


def solution(mesh):
    in_specs = (
        P(None, "modes", "space", None),
        P(None, "modes", "space", None),
        P("space", None),
        P(),
        P(),
        P(),
        P(),
        P("modes", None, None),
    )
    out_specs = P(None, "modes", "space", None)
    return jax.shard_map(body, mesh=mesh, in_specs=in_specs, out_specs=out_specs, check_vma=False)
```

profile of v0, /device:TPU:56, one launch (start us, length us, event | category | flops | bytes accessed | tf_op | source)
XLA Modules:
  0.0 182.5 jit_solution(13610392275170002387)
XLA Ops:
  0.0 1.4 fusion.72
  1.5 1.9 %collective-permute-start.1 = (f32[2,16,1,512]{3,1,2,0:T(8,128)S(1)}, f32[2,16,1,512]{3,1,2,0:T(8,128)S(1)}, u32[]{:S(2)}, u32[]{:S(2)}) collective-permute-start(f32[2,16,1,512]{3,1,2,0:T(8,128)S(1)} %get-tuple-element.22), channel_id=1, source_target_pairs={{0,16},{16,32},{32,48},{48,64},{64,80},{80,96},{96,112},{112,128},... | collective-permute-start | bytes 196616 | tf_op jit(solution)/shard_map/ppermute | solution.py:15
  3.4 4.5 %collective-permute-start = (f32[2,16,1,512]{3,1,2,0:T(8,128)S(1)}, f32[2,16,1,512]{3,1,2,0:T(8,128)S(1)}, u32[]{:S(2)}, u32[]{:S(2)}) collective-permute-start(f32[2,16,1,512]{3,1,2,0:T(8,128)S(1)} %get-tuple-element.21), channel_id=1, source_target_pairs={{16,0},{32,16},{48,32},{64,48},{80,64},{96,80},{112,96},{128,112},... | collective-permute-start | bytes 196616 | tf_op jit(solution)/shard_map/ppermute | solution.py:18
  8.1 0.1 copy.73
  8.2 0.1 copy.74
  8.3 0.1 copy.75
  8.4 0.1 copy.76
  8.5 0.1 copy.77
  8.6 0.1 copy.78
  8.7 0.1 copy.79
  8.9 0.4 multiply_add_fusion
  9.3 0.5 collective-permute-done
  9.9 0.4 fusion.71
  10.4 0.1 convert_element_type.108
  10.6 1.6 multiply_convert_fusion.1
  12.2 13.0 %all-to-all-start = ((bf16[2,3,16,16,512]{4,2,1,0,3:T(8,128)(2,1)}), bf16[2,3,16,16,512]{4,2,1,0,3:T(8,128)(2,1)S(1)}, u32[]{:S(2)}, u32[]{:S(2)}) async-start(bf16[2,3,16,16,512]{4,2,1,0,3:T(8,128)(2,1)} %multiply_convert_fusion.1), calls=%async_computation | async-start | bytes 3145728 | tf_op jit(solution)/shard_map/all_to_all | solution.py:58
  25.3 2.1 %mul.509 = bf16[3,16,16,16,16]{4,3,2,1,0:T(8,128)(2,1)} broadcast(bf16[3,16,16]{2,1,0:T(8,128)(2,1)S(1)} %convert_element_type.110), dimensions={0,1,3} | broadcast | bytes 394752 | tf_op jit(solution)/shard_map/mul | solution.py:44
  27.4 4.4 %mul.510 = bf16[3,256,256]{2,1,0:T(8,128)(2,1)S(1)} reshape(bf16[3,16,16,16,16]{4,3,2,1,0:T(8,128)(2,1)} %mul.509) | data formatting | bytes 786432 | tf_op jit(solution)/shard_map/mul | solution.py:44
  31.8 34.9 %all-to-all-done = bf16[2,3,16,16,512]{4,2,1,0,3:T(8,128)(2,1)S(1)} async-done(((bf16[2,3,16,16,512]{4,2,1,0,3:T(8,128)(2,1)}), bf16[2,3,16,16,512]{4,2,1,0,3:T(8,128)(2,1)S(1)}, u32[]{:S(2)}, u32[]{:S(2)}) %all-to-all-start) | async-done | bytes 1572896 | tf_op jit(solution)/shard_map/all_to_all | solution.py:58
  66.7 0.1 copy.83
  66.9 0.9 copy-done.21
  67.7 0.6 fusion.7
  68.4 1.2 copy.85
  69.6 3.6 %all-to-all-start.1 = ((bf16[2,256,1,512]{3,0,2,1:T(2,128)(2,1)}), bf16[2,256,1,512]{3,0,2,1:T(2,128)(2,1)S(1)}, u32[]{:S(2)}, u32[]{:S(2)}) async-start(bf16[2,256,1,512]{3,0,2,1:T(2,128)(2,1)} %copy.85), calls=%async_computation.1 | async-start | bytes 1048576 | tf_op jit(solution)/shard_map/all_to_all | solution.py:59
  73.2 0.3 slice_reduce_fusion.7
  73.5 0.1 multiply_divide_fusion
  73.6 1.4 fusion.68
  75.0 17.1 %all-to-all-done.1 = bf16[2,256,1,512]{3,0,2,1:T(2,128)(2,1)S(1)} async-done(((bf16[2,256,1,512]{3,0,2,1:T(2,128)(2,1)}), bf16[2,256,1,512]{3,0,2,1:T(2,128)(2,1)S(1)}, u32[]{:S(2)}, u32[]{:S(2)}) %all-to-all-start.1) | async-done | bytes 524320 | tf_op jit(solution)/shard_map/all_to_all | solution.py:59
  92.1 3.3 %fusion.74 = (bf16[2,16,16,512]{3,1,2,0:T(8,128)(2,1)S(1)}, f32[2,16,16,512]{3,1,2,0:T(8,128)S(1)}) fusion(f32[2,16,16,512]{3,1,2,0:T(8,128)S(1)} %get-tuple-element.28, f32[1,16,16]{2,1,0:T(8,128)S(1)} %copy-done, f32[2,16,1,512]{3,1,2,0:T(8,128)} %copy-done.11, f32[2,16,1,512]{3,1,2,0:T(8,128)} %copy-done.12, ...), kind=kOutput, calls=%fused_computation.108 | convolution fusion | flops 54525952 | bytes 6026240 | tf_op jit(solution)/shard_map/bac,fbcxy->fbaxy/dot_general | solution.py:72
  95.5 1.9 %collective-permute-start.3 = (f32[2,16,1,512]{3,1,2,0:T(8,128)S(1)}, f32[2,16,1,512]{3,1,2,0:T(8,128)S(1)}, u32[]{:S(2)}, u32[]{:S(2)}) collective-permute-start(f32[2,16,1,512]{3,1,2,0:T(8,128)S(1)} %get-tuple-element.18), channel_id=1, source_target_pairs={{0,16},{16,32},{32,48},{48,64},{64,80},{80,96},{96,112},{112,128},... | collective-permute-start | bytes 196616 | tf_op jit(solution)/shard_map/ppermute | solution.py:15
  97.4 4.5 %collective-permute-start.2 = (f32[2,16,1,512]{3,1,2,0:T(8,128)S(1)}, f32[2,16,1,512]{3,1,2,0:T(8,128)S(1)}, u32[]{:S(2)}, u32[]{:S(2)}) collective-permute-start(f32[2,16,1,512]{3,1,2,0:T(8,128)S(1)} %get-tuple-element.17), channel_id=1, source_target_pairs={{16,0},{32,16},{48,32},{64,48},{80,64},{96,80},{112,96},{128,112},... | collective-permute-start | bytes 196616 | tf_op jit(solution)/shard_map/ppermute | solution.py:18
  102.0 1.8 %collective-permute-done.2 = f32[2,16,1,512]{3,1,2,0:T(8,128)S(1)} collective-permute-done((f32[2,16,1,512]{3,1,2,0:T(8,128)S(1)}, f32[2,16,1,512]{3,1,2,0:T(8,128)S(1)}, u32[]{:S(2)}, u32[]{:S(2)}) %collective-permute-start.2) | collective-permute-done | bytes 65568 | tf_op jit(solution)/shard_map/ppermute | solution.py:18
  103.9 0.6 copy-done.15
  104.5 0.4 fusion.70
  104.9 0.1 convert_element_type.118
  105.1 0.5 multiply_convert_fusion
  105.6 45.6 %all_to_all.48 = bf16[2,3,16,16,512]{4,2,1,0,3:T(8,128)(2,1)S(1)} all-to-all(bf16[2,3,16,16,512]{4,2,1,0,3:T(8,128)(2,1)S(1)} %multiply_convert_fusion), channel_id=1, replica_groups=mesh['space'=32,'modes'=16] {'modes'}, dimensions={3} | all-to-all | bytes 3145728 | tf_op jit(solution)/shard_map/all_to_all | solution.py:58
  151.1 0.2 copy.88
  151.3 0.8 copy-done.2
  152.1 0.1 copy-done.22
  152.3 0.7 fusion.6
  152.9 1.2 copy.90
  154.1 4.4 %all-to-all-start.3 = ((bf16[2,256,1,512]{3,0,2,1:T(2,128)(2,1)}), bf16[2,256,1,512]{3,0,2,1:T(2,128)(2,1)}, u32[]{:S(2)}, u32[]{:S(2)}) async-start(bf16[2,256,1,512]{3,0,2,1:T(2,128)(2,1)} %copy.90), calls=%async_computation.3 | async-start | bytes 1048576 | tf_op jit(solution)/shard_map/all_to_all | solution.py:59
  158.5 0.4 fusion.66
  158.9 17.9 %all-to-all-done.3 = bf16[2,256,1,512]{3,0,2,1:T(2,128)(2,1)} async-done(((bf16[2,256,1,512]{3,0,2,1:T(2,128)(2,1)}), bf16[2,256,1,512]{3,0,2,1:T(2,128)(2,1)}, u32[]{:S(2)}, u32[]{:S(2)}) %all-to-all-start.3) | async-done | bytes 524320 | tf_op jit(solution)/shard_map/all_to_all | solution.py:59
  176.9 1.1 copy.91
  178.0 2.9 %fusion.1 = f32[2,16,16,512]{3,1,2,0:T(8,128)S(1)} fusion(f32[2,16,16,512]{3,1,2,0:T(8,128)S(1)} %get-tuple-element.46, f32[2,16,1,512]{3,1,2,0:T(8,128)S(1)} %copy-done.14, f32[2,16,1,512]{3,1,2,0:T(8,128)S(1)} %copy-done.16, bf16[2,16,16,1,512]{4,2,1,0,3:T(8,128)(2,1)S(1)} %bitcast.97, f32[2,16,16,511]{3,1,2,0:T(8,128)S(1)} %get-tuple-element.16, ...), kind=kOutput, calls=%fused_computation.4 | convolution fusion | flops 54263808 | bytes 5501952 | tf_op jit(solution)/shard_map/bac,fbcxy->fbaxy/dot_general | solution.py:72
  181.0 1.6 copy.92
  (57 shorter events, 0.6 us)
Async XLA Ops:
  0.0 92.1 %copy-start = (f32[1,16,16]{2,1,0:T(8,128)S(1)}, f32[1,16,16]{2,1,0:T(8,128)}, u32[]{:S(2)}) copy-start(f32[1,16,16]{2,1,0:T(8,128)} %param.15) | copy-start | bytes 3076
  0.0 7.9 %copy-start.19 = (s32[16,512]{1,0:T(8,128)S(1)}, s32[16,512]{1,0:T(8,128)}, u32[]{:S(2)}) copy-start(s32[16,512]{1,0:T(8,128)} %param.10) | copy-start | bytes 98308
  0.0 8.0 %copy-start.17 = (f32[2,3,8]{2,0,1:T(2,128)S(1)}, f32[2,3,8]{2,0,1:T(2,128)}, u32[]{:S(2)}) copy-start(f32[2,3,8]{2,0,1:T(2,128)} %param.12) | copy-start | bytes 580
  1.5 7.8 %collective-permute-start.1 = (f32[2,16,1,512]{3,1,2,0:T(8,128)S(1)}, f32[2,16,1,512]{3,1,2,0:T(8,128)S(1)}, u32[]{:S(2)}, u32[]{:S(2)}) collective-permute-start(f32[2,16,1,512]{3,1,2,0:T(8,128)S(1)} %get-tuple-element.22), channel_id=1, source_target_pairs={{0,16},{16,32},{32,48},{48,64},{64,80},{80,96},{96,112},{112,128},... | collective-permute-start | bytes 196616 | tf_op jit(solution)/shard_map/ppermute | solution.py:15
  3.4 6.4 %collective-permute-start = (f32[2,16,1,512]{3,1,2,0:T(8,128)S(1)}, f32[2,16,1,512]{3,1,2,0:T(8,128)S(1)}, u32[]{:S(2)}, u32[]{:S(2)}) collective-permute-start(f32[2,16,1,512]{3,1,2,0:T(8,128)S(1)} %get-tuple-element.21), channel_id=1, source_target_pairs={{16,0},{32,16},{48,32},{64,48},{80,64},{96,80},{112,96},{128,112},... | collective-permute-start | bytes 196616 | tf_op jit(solution)/shard_map/ppermute | solution.py:18
  8.0 2.3 %copy-start.3 = (f32[16,512]{1,0:T(8,128)}, f32[16,512]{1,0:T(8,128)S(1)}, u32[]{:S(2)}) copy-start(f32[16,512]{1,0:T(8,128)S(1)} %get-tuple-element.33) | copy-start | bytes 98308
  8.0 2.3 %copy-start.5 = (f32[16,512]{1,0:T(8,128)}, f32[16,512]{1,0:T(8,128)S(1)}, u32[]{:S(2)}) copy-start(f32[16,512]{1,0:T(8,128)S(1)} %get-tuple-element.34) | copy-start | bytes 98308
  8.0 2.3 %copy-start.7 = (f32[16,512]{1,0:T(8,128)}, f32[16,512]{1,0:T(8,128)S(1)}, u32[]{:S(2)}) copy-start(f32[16,512]{1,0:T(8,128)S(1)} %get-tuple-element.35) | copy-start | bytes 98308
  8.0 2.3 %copy-start.9 = (f32[16,512]{1,0:T(8,128)}, f32[16,512]{1,0:T(8,128)S(1)}, u32[]{:S(2)}) copy-start(f32[16,512]{1,0:T(8,128)S(1)} %get-tuple-element.36) | copy-start | bytes 98308
  9.3 1.1 copy-start.11
  9.8 0.6 copy-start.12
  12.2 13.0 %copy-start.20 = (s32[3,16,16]{2,1,0:T(8,128)S(1)}, s32[3,16,16]{2,1,0:T(8,128)}, u32[]{:S(2)}) copy-start(s32[3,16,16]{2,1,0:T(8,128)} %param.14) | copy-start | bytes 9220
  12.2 54.5 %all-to-all-start = ((bf16[2,3,16,16,512]{4,2,1,0,3:T(8,128)(2,1)}), bf16[2,3,16,16,512]{4,2,1,0,3:T(8,128)(2,1)S(1)}, u32[]{:S(2)}, u32[]{:S(2)}) async-start(bf16[2,3,16,16,512]{4,2,1,0,3:T(8,128)(2,1)} %multiply_convert_fusion.1), calls=%async_computation | async-start | bytes 3145728 | tf_op jit(solution)/shard_map/all_to_all | solution.py:58
  31.8 35.1 %copy-start.1 = (bf16[3,256,256]{2,1,0:T(8,128)(2,1)}, bf16[3,256,256]{2,1,0:T(8,128)(2,1)S(1)}, u32[]{:S(2)}) copy-start(bf16[3,256,256]{2,1,0:T(8,128)(2,1)S(1)} %mul.510) | copy-start | bytes 1179652
  66.7 1.0 copy-start.21
  68.4 4.8 %copy-start.18 = (f32[2,8]{1,0:T(2,128)S(1)}, f32[2,8]{1,0:T(2,128)}, u32[]{:S(2)}) copy-start(f32[2,8]{1,0:T(2,128)} %param.11) | copy-start | bytes 196
  68.4 5.1 %copy-start.4 = (f32[16,512]{1,0:T(8,128)S(1)}, f32[16,512]{1,0:T(8,128)}, u32[]{:S(2)}) copy-start(f32[16,512]{1,0:T(8,128)} %copy-done.3) | copy-start | bytes 98308
  68.4 5.1 %copy-start.6 = (f32[16,512]{1,0:T(8,128)S(1)}, f32[16,512]{1,0:T(8,128)}, u32[]{:S(2)}) copy-start(f32[16,512]{1,0:T(8,128)} %copy-done.5) | copy-start | bytes 98308
  68.4 5.1 %copy-start.8 = (f32[16,512]{1,0:T(8,128)S(1)}, f32[16,512]{1,0:T(8,128)}, u32[]{:S(2)}) copy-start(f32[16,512]{1,0:T(8,128)} %copy-done.7) | copy-start | bytes 98308
  68.4 5.1 %copy-start.10 = (f32[16,512]{1,0:T(8,128)S(1)}, f32[16,512]{1,0:T(8,128)}, u32[]{:S(2)}) copy-start(f32[16,512]{1,0:T(8,128)} %copy-done.9) | copy-start | bytes 98308
  69.6 22.5 %all-to-all-start.1 = ((bf16[2,256,1,512]{3,0,2,1:T(2,128)(2,1)}), bf16[2,256,1,512]{3,0,2,1:T(2,128)(2,1)S(1)}, u32[]{:S(2)}, u32[]{:S(2)}) async-start(bf16[2,256,1,512]{3,0,2,1:T(2,128)(2,1)} %copy.85), calls=%async_computation.1 | async-start | bytes 1048576 | tf_op jit(solution)/shard_map/all_to_all | solution.py:59
  95.5 6.5 %collective-permute-start.3 = (f32[2,16,1,512]{3,1,2,0:T(8,128)S(1)}, f32[2,16,1,512]{3,1,2,0:T(8,128)S(1)}, u32[]{:S(2)}, u32[]{:S(2)}) collective-permute-start(f32[2,16,1,512]{3,1,2,0:T(8,128)S(1)} %get-tuple-element.18), channel_id=1, source_target_pairs={{0,16},{16,32},{32,48},{48,64},{64,80},{80,96},{96,112},{112,128},... | collective-permute-start | bytes 196616 | tf_op jit(solution)/shard_map/ppermute | solution.py:15
  97.4 6.4 %collective-permute-start.2 = (f32[2,16,1,512]{3,1,2,0:T(8,128)S(1)}, f32[2,16,1,512]{3,1,2,0:T(8,128)S(1)}, u32[]{:S(2)}, u32[]{:S(2)}) collective-permute-start(f32[2,16,1,512]{3,1,2,0:T(8,128)S(1)} %get-tuple-element.17), channel_id=1, source_target_pairs={{16,0},{32,16},{48,32},{64,48},{80,64},{96,80},{112,96},{128,112},... | collective-permute-start | bytes 196616 | tf_op jit(solution)/shard_map/ppermute | solution.py:18
  102.0 1.9 %copy-start.13 = (f32[2,16,1,512]{3,1,2,0:T(8,128)}, f32[2,16,1,512]{3,1,2,0:T(8,128)S(1)}, u32[]{:S(2)}) copy-start(f32[2,16,1,512]{3,1,2,0:T(8,128)S(1)} %collective-permute-done.3) | copy-start | bytes 196612
  103.9 0.6 copy-start.15
  151.1 1.0 copy-start.2
  151.1 1.1 copy-start.22
  154.1 22.8 %all-to-all-start.3 = ((bf16[2,256,1,512]{3,0,2,1:T(2,128)(2,1)}), bf16[2,256,1,512]{3,0,2,1:T(2,128)(2,1)}, u32[]{:S(2)}, u32[]{:S(2)}) async-start(bf16[2,256,1,512]{3,0,2,1:T(2,128)(2,1)} %copy.90), calls=%async_computation.3 | async-start | bytes 1048576 | tf_op jit(solution)/shard_map/all_to_all | solution.py:59
  158.5 19.5 %copy-start.14 = (f32[2,16,1,512]{3,1,2,0:T(8,128)S(1)}, f32[2,16,1,512]{3,1,2,0:T(8,128)}, u32[]{:S(2)}) copy-start(f32[2,16,1,512]{3,1,2,0:T(8,128)} %copy-done.13) | copy-start | bytes 196612
  158.5 19.5 %copy-start.16 = (f32[2,16,1,512]{3,1,2,0:T(8,128)S(1)}, f32[2,16,1,512]{3,1,2,0:T(8,128)}, u32[]{:S(2)}) copy-start(f32[2,16,1,512]{3,1,2,0:T(8,128)} %copy-done.15) | copy-start | bytes 196612
where the time goes:
time: 183 us
  waiting for transfers between devices  72.3 us (40%)
  blocking collectives  45.6 us (25%)
  starting transfers between devices  33.9 us (19%)
  local copies, waits for them, and re-layouts  18.1 us (10%)
  matrix products  7.58 us (4%)
  other arithmetic  4.48 us (2%)
    all_to_all x1, blocking collectives, body(): lax.all_to_all(tiles, 'modes', split_axis=3, concat_axis=2, tiled=True)  45.6 us
    all_to_all x2, waiting for transfers between devices, body(): lax.all_to_all(jnp.einsum('kij,fkjxy->fixy', coupling, mix_tiles, preferr...  35 us
    all_to_all x1, waiting for transfers between devices, body(): lax.all_to_all(tiles, 'modes', split_axis=3, concat_axis=2, tiled=True)  34.9 us
    all_to_all x1, starting transfers between devices, body(): lax.all_to_all(tiles, 'modes', split_axis=3, concat_axis=2, tiled=True)  13 us
    ppermute x2, starting transfers between devices, with_halo(): lax.ppermute(lax.slice_in_dim(block, 0, width, axis=dim), axis, backward)  9.08 us
    all_to_all x2, starting transfers between devices, body(): lax.all_to_all(jnp.einsum('kij,fkjxy->fixy', coupling, mix_tiles, preferr...  7.99 us
    mul x2, local copies, waits for them, and re-layouts, body(): shaped * block_mask[:, :, None, :, None].astype(jnp.bfloat16)  6.52 us
    dot_general x2, matrix products, body(): jnp.einsum('bac,fbcxy->fbaxy', block_inverse, grouped, precision=lax.Prec...  6.28 us
  transfers between devices with their start and end apart: 7, of which 5 were waited for; matrix products, arithmetic and copies ran while one was open for 5% of the time, Pallas kernels for 0%

commit v1 on v0

v1 whole, which is shorter than its diff:
```python
import jax
import jax.numpy as jnp
from jax import lax
from jax.sharding import PartitionSpec as P

SWEEPS = 2
LANES = 128


def ring_halo(block, axis, dim):
    count = lax.axis_size(axis)
    forward = [(i, (i + 1) % count) for i in range(count)]
    backward = [(target, source) for source, target in forward]
    low = lax.ppermute(lax.slice_in_dim(block, block.shape[dim] - 1, None, axis=dim), axis, forward)
    high = lax.ppermute(lax.slice_in_dim(block, 0, 1, axis=dim), axis, backward)
    return jnp.concatenate([low, block, high], axis=dim)


def lookup(table, region):
    total = jnp.zeros(table.shape[:-1] + region.shape, jnp.float32)
    for which in range(table.shape[-1]):
        total = total + table[..., which, None, None] * (region == which).astype(jnp.float32)
    return total


def shift_lanes(center, fill_left, fill_right):
    right = jnp.concatenate([center[..., 1:], fill_right[..., None]], -1)
    left = jnp.concatenate([fill_left[..., None], center[..., :-1]], -1)
    return right, left


def body(rhs, initial, region, base_table, term_table, galerkin, block_mask, block_inverse):
    terms = galerkin.shape[0]
    modes_all = galerkin.shape[1]
    blocks = block_mask.shape[1]
    width = modes_all // blocks
    shaped = galerkin.reshape(terms, blocks, width, blocks, width)
    coupling = (shaped * block_mask[:, :, None, :, None].astype(jnp.bfloat16)).reshape(
        terms, modes_all, modes_all
    )
    coupling = coupling.transpose(1, 0, 2).reshape(modes_all, terms * modes_all)

    fields = rhs.shape[0]
    rows, cols = region.shape
    devs = lax.axis_size("modes")
    col_chunks = cols // LANES
    row_chunks = devs // col_chunks
    rows_c = rows // row_chunks
    me = lax.axis_index("modes")
    my_r = me // col_chunks
    my_c = me % col_chunks

    base = lookup(base_table, region)[:, :, None, :]
    coef = lookup(term_table, region)
    coef_chunk = lax.dynamic_slice(
        coef, (0, 0, my_r * rows_c, my_c * LANES), (fields, terms, rows_c, LANES)
    )
    coef_chunk = coef_chunk.transpose(0, 2, 1, 3)[:, :, :, None, :]
    rhs_x = rhs.transpose(0, 2, 1, 3).astype(jnp.float32)
    inverse_base = 1.0 / (4.0 * base)
    u_field = initial.transpose(0, 2, 1, 3).astype(jnp.float32)
    inv = block_inverse[0]
    zero_col = jnp.zeros(u_field.shape[:1] + (rows_c,) + u_field.shape[2:3], jnp.bfloat16)
    for sweep in range(SWEEPS):
        padded = ring_halo(u_field, "space", 1)
        center = padded[:, 1:-1]
        zeros = jnp.zeros(center.shape[:-1], jnp.float32)
        right, left = shift_lanes(center, zeros, zeros)
        local = base * (4.0 * center - padded[:, 2:] - padded[:, :-2] - right - left)

        rounded = padded.astype(jnp.bfloat16)
        pieces = []
        for r in range(row_chunks):
            for c in range(col_chunks):
                main = rounded[:, r * rows_c : r * rows_c + rows_c + 2, :, c * LANES : (c + 1) * LANES]
                inner = rounded[:, r * rows_c + 1 : r * rows_c + rows_c + 1]
                hl = inner[..., c * LANES - 1] if c > 0 else zero_col
                hr = inner[..., (c + 1) * LANES] if c < col_chunks - 1 else zero_col
                side = jnp.concatenate([hl, hr], axis=1).transpose(0, 2, 1)
                side = jnp.pad(side, ((0, 0), (0, 0), (0, LANES - 2 * rows_c)))[:, None]
                pieces.append(jnp.concatenate([main, side], axis=1))
        stacked = jnp.stack(pieces, axis=2)
        got = lax.all_to_all(stacked, "modes", split_axis=2, concat_axis=3, tiled=True)
        got = got[:, :, 0].astype(jnp.float32)
        g_center = got[:, 1 : rows_c + 1]
        side = got[:, rows_c + 2]
        g_left = side[..., :rows_c].transpose(0, 2, 1)
        g_right = side[..., rows_c : 2 * rows_c].transpose(0, 2, 1)
        g_r, g_l = shift_lanes(g_center, g_left, g_right)
        lap = 4.0 * g_center - got[:, 2 : rows_c + 2] - got[:, 0:rows_c] - g_r - g_l
        tiles = (coef_chunk * lap[:, :, None]).astype(jnp.bfloat16)
        tiles = tiles.reshape(fields, rows_c, terms * modes_all, LANES)
        mixed = jnp.einsum(
            "ic,fxcy->fxiy", coupling, tiles, preferred_element_type=jnp.float32
        ).astype(jnp.bfloat16)
        mixed = mixed.reshape(fields, rows_c, devs, modes_all // devs, LANES)
        back = lax.all_to_all(mixed, "modes", split_axis=2, concat_axis=2, tiled=True)
        back = back.reshape(fields, rows_c, row_chunks, col_chunks, -1, LANES)
        coupled = back.transpose(0, 2, 1, 4, 3, 5).reshape(u_field.shape)

        resid = rhs_x - local - coupled.astype(jnp.float32)
        scaled = resid * inverse_base
        update = jnp.einsum("ac,fxcy->fxay", inv, scaled, precision=lax.Precision.HIGHEST)
        u_field = u_field + 0.6 * update
    return u_field.transpose(0, 2, 1, 3)


def solution(mesh):
    in_specs = (
        P(None, "modes", "space", None),
        P(None, "modes", "space", None),
        P("space", None),
        P(),
        P(),
        P(),
        P(),
        P("modes", None, None),
    )
    out_specs = P(None, "modes", "space", None)
    return jax.shard_map(body, mesh=mesh, in_specs=in_specs, out_specs=out_specs, check_vma=False)
```

time: 183 us -> 217 us (1.19); the launches traced: 183 us -> 214 us
  local copies, waits for them, and re-layouts: 18.1 us -> 69.3 us
  waiting for transfers between devices: 72.3 us -> 49.8 us
  other arithmetic: 4.48 us -> 21.1 us
  blocking collectives: 45.6 us -> 31.8 us
  starting transfers between devices: 33.9 us -> 31 us
  matrix products: 7.58 us -> 10.4 us
    broadcast_in_dim x0 -> x38, local copies, waits for them, and re-layouts: none -> 20.9 us  [the longest x4 10.4 us: shift_lanes(): left = jnp.concatenate([fill_left[..., None], center[..., :-1]], -1)]
    all_to_all x3, waiting for transfers between devices: 69.9 us -> 49.7 us  [the longest x2 31.3 us: body(): lax.all_to_all(mixed, 'modes', split_axis=2, concat_axis=2, tiled=True)]
    squeeze x0 -> x50, local copies, waits for them, and re-layouts: none -> 15.1 us  [the longest x24 7.54 us: body(): hr = inner[..., (c + 1) * LANES] if c < col_chunks - 1 else zero_col]
    all_to_all x1, blocking collectives: 45.6 us -> 31.8 us  [body(): lax.all_to_all(stacked, 'modes', split_axis=2, concat_axis=3, tiled=True)]
    unnamed x1 -> x30, other arithmetic: 1.44 us -> 9.68 us
    sub x0 -> x2, other arithmetic: none -> 7.55 us  [body(): lap = 4.0 * g_center - got[:, 2:rows_c + 2] - got[:, 0:rows_c] - g_r - g_l]
    slice x6 -> x12, local copies, waits for them, and re-layouts: 2.53 us -> 8.14 us  [the longest x2 3.39 us: shift_lanes(): right = jnp.concatenate([center[..., 1:], fill_right[..., None]], -1)]
    convert_element_type x2 -> x8, local copies, waits for them, and re-layouts: 2.34 us -> 7.9 us  [the longest x4 5.82 us: body(): resid = rhs_x - local - coupled.astype(jnp.float32)]
  transfers between devices with their start and end apart: 7 -> 7, of which waited for: 5 -> 3; matrix products, arithmetic and copies ran while one was open for 5% -> 18% of each run, Pallas kernels for 0% -> 0%
where the time goes in v1:
time: 217 us; the launch traced here: 214 us
  local copies, waits for them, and re-layouts  69.3 us (32%)
  waiting for transfers between devices  49.8 us (23%)
  blocking collectives  31.8 us (15%)
  starting transfers between devices  31 us (14%)
  other arithmetic  21.1 us (10%)
  matrix products  10.4 us (5%)
    all_to_all x1, blocking collectives, body(): lax.all_to_all(stacked, 'modes', split_axis=2, concat_axis=3, tiled=True)  31.8 us
    all_to_all x2, waiting for transfers between devices, body(): lax.all_to_all(mixed, 'modes', split_axis=2, concat_axis=2, tiled=True)  31.3 us
    all_to_all x1, waiting for transfers between devices, body(): lax.all_to_all(stacked, 'modes', split_axis=2, concat_axis=3, tiled=True)  18.4 us
    all_to_all x1, starting transfers between devices, body(): lax.all_to_all(stacked, 'modes', split_axis=2, concat_axis=3, tiled=True)  12.6 us
    broadcast_in_dim x4, local copies, waits for them, and re-layouts, shift_lanes(): left = jnp.concatenate([fill_left[..., None], center[..., :-1]], -1)  10.4 us
    broadcast_in_dim x2, local copies, waits for them, and re-layouts, shift_lanes(): right = jnp.concatenate([center[..., 1:], fill_right[..., None]], -1)  10.3 us
    unnamed x30, other arithmetic  9.68 us
    dot_general x2, matrix products, body(): jnp.einsum('ac,fxcy->fxay', inv, scaled, precision=lax.Precision.HIGHEST)  9.11 us
  transfers between devices with their start and end apart: 7, of which 3 were waited for; matrix products, arithmetic and copies ran while one was open for 18% of the time, Pallas kernels for 0%

profile of v1, /device:TPU:56, one launch (start us, length us, event | category | flops | bytes accessed | tf_op | source)
XLA Modules:
  0.0 214.3 jit_solution(13734791047378023993)
XLA Ops:
  0.0 1.4 fusion.126
  1.4 3.6 %collective-permute-start = (f32[2,1,16,512]{3,2,1,0:T(8,128)S(1)}, f32[2,1,16,512]{3,2,1,0:T(8,128)S(1)}, u32[]{:S(2)}, u32[]{:S(2)}) collective-permute-start(f32[2,1,16,512]{3,2,1,0:T(8,128)S(1)} %get-tuple-element.27), channel_id=1, source_target_pairs={{16,0},{32,16},{48,32},{64,48},{80,64},{96,80},{112,96},{128,112},... | collective-permute-start | bytes 196616 | tf_op jit(solution)/shard_map/ppermute | solution.py:15
  5.1 1.9 collective-permute-start.1
  16.2 0.6 constant_dynamic-update-slice_fusion.15
  16.8 0.6 constant_dynamic-update-slice_fusion.14
  17.4 0.6 constant_dynamic-update-slice_fusion.13
  18.1 0.6 constant_dynamic-update-slice_fusion.12
  18.7 0.6 constant_dynamic-update-slice_fusion.11
  23.7 0.6 constant_dynamic-update-slice_fusion.3
  24.4 0.6 constant_dynamic-update-slice_fusion.2
  25.0 0.6 constant_dynamic-update-slice_fusion.1
  25.6 0.6 constant_dynamic-update-slice_fusion
  26.3 12.6 %all-to-all-start = ((bf16[2,7,16,16,128]{4,3,1,0,2:T(8,128)(2,1)}), bf16[2,7,16,16,128]{4,3,1,0,2:T(8,128)(2,1)}, u32[]{:S(2)}, u32[]{:S(2)}) async-start(bf16[2,7,16,16,128]{4,3,1,0,2:T(8,128)(2,1)} %constant_dynamic-update-slice_fusion), calls=%async_computation | async-start | bytes 1835008 | tf_op jit(solution)/shard_map/all_to_all | solution.py:83
  40.9 2.1 mul.478
  43.0 5.1 %mul.479 = bf16[3,256,256]{2,1,0:T(8,128)(2,1)} reshape(bf16[3,16,16,16,16]{4,3,2,1,0:T(8,128)(2,1)} %mul.478) | data formatting | bytes 786432 | tf_op jit(solution)/shard_map/mul | solution.py:38
  48.4 18.4 %all-to-all-done = bf16[2,7,16,16,128]{4,3,1,0,2:T(8,128)(2,1)} async-done(((bf16[2,7,16,16,128]{4,3,1,0,2:T(8,128)(2,1)}), bf16[2,7,16,16,128]{4,3,1,0,2:T(8,128)(2,1)}, u32[]{:S(2)}, u32[]{:S(2)}) %all-to-all-start) | async-done | bytes 917536 | tf_op jit(solution)/shard_map/all_to_all | solution.py:83
  66.8 1.4 copy.329
  68.2 1.7 fusion.129
  70.0 4.6 %copy.333 = f32[2,4,256,1]{3,2,1,0:T(8,128)} copy(f32[2,4,256,1]{1,2,0,3:T(8,128)S(1)} %get-tuple-element.97) | data formatting | bytes 16384 | tf_op jit(solution)/shard_map/broadcast_in_dim | solution.py:28
  74.7 4.6 %copy.331 = f32[2,4,256,1]{3,2,1,0:T(8,128)} copy(f32[2,4,256,1]{1,2,0,3:T(8,128)S(1)} %get-tuple-element.98) | data formatting | bytes 16384 | tf_op jit(solution)/shard_map/broadcast_in_dim | solution.py:27
  79.3 3.9 %fusion.29 = f32[2,4,256,128]{3,2,1,0:T(8,128)} fusion(f32[2,7,256,128]{3,2,1,0:T(8,128)S(1)} %bitcast.418, f32[2,4,256,1]{3,2,1,0:T(8,128)} %copy.331, f32[2,4,256,127]{3,2,1,0:T(8,128)} %get-tuple-element.20, f32[2,4,256,127]{3,2,1,0:T(8,128)} %get-tuple-element.19, f32[2,4,256,1]{3,2,1,0:T(8,128)} %copy.333), kind=kLoop, calls=%fused_computation.37 | loop fusion | flops 1835008 | bytes 6291456 | tf_op jit(solution)/shard_map/sub | solution.py:90
  83.2 1.6 copy.334
  84.9 0.6 fusion.13
  85.9 0.9 copy.336
  86.8 3.8 %all-to-all-start.1 = ((bf16[2,4,16,16,128]{4,3,1,0,2:T(8,128)(2,1)}), bf16[2,4,16,16,128]{4,3,1,0,2:T(8,128)(2,1)S(1)}, u32[]{:S(2)}, u32[]{:S(2)}) async-start(bf16[2,4,16,16,128]{4,3,1,0,2:T(8,128)(2,1)} %copy.336), calls=%async_computation.1 | async-start | bytes 1048576 | tf_op jit(solution)/shard_map/all_to_all | solution.py:97
  91.0 1.7 fusion.132
  92.7 15.6 %all-to-all-done.1 = bf16[2,4,16,16,128]{4,3,1,0,2:T(8,128)(2,1)S(1)} async-done(((bf16[2,4,16,16,128]{4,3,1,0,2:T(8,128)(2,1)}), bf16[2,4,16,16,128]{4,3,1,0,2:T(8,128)(2,1)S(1)}, u32[]{:S(2)}, u32[]{:S(2)}) %all-to-all-start.1) | async-done | bytes 524320 | tf_op jit(solution)/shard_map/all_to_all | solution.py:97
  108.8 1.4 reshape.95
  110.2 5.1 %fusion.127 = (bf16[2,16,16,512]{3,2,1,0:T(8,128)(2,1)S(1)}, f32[2,16,16,512]{3,2,1,0:T(8,128)S(1)}, f32[2,16,512,16]{2,3,1,0:T(8,128)}) fusion(bf16[2,16,16,512]{3,2,1,0:T(8,128)(2,1)S(1)} %copy-done.3, f32[1,16,16]{2,1,0:T(8,128)S(1)} %copy-done, f32[2,16,16,512]{3,2,1,0:T(8,128)} %reshape.95, f32[2,16,16,512]{3,2,1,0:T(8,128)S(1)} %get-tuple-element.93, ...), kind=kOutput, calls=%fused_computation.290 | convolution fusion | flops 54525952 | bytes 8123392 | tf_op jit(solution)/shard_map/ac,fxcy->fxay/dot_general | solution.py:103
  115.6 0.7 fusion.131
  116.3 3.4 %collective-permute-start.2 = (f32[2,1,16,512]{3,2,1,0:T(8,128)}, f32[2,1,16,512]{3,2,1,0:T(8,128)S(1)}, u32[]{:S(2)}, u32[]{:S(2)}) collective-permute-start(f32[2,1,16,512]{3,2,1,0:T(8,128)} %get-tuple-element.23), channel_id=1, source_target_pairs={{16,0},{32,16},{48,32},{64,48},{80,64},{96,80},{112,96},{128,112},... | collective-permute-start | bytes 196616 | tf_op jit(solution)/shard_map/ppermute | solution.py:15
  119.7 1.9 collective-permute-start.3
  131.3 31.8 %all_to_all.28 = bf16[2,7,16,16,128]{4,3,1,0,2:T(8,128)(2,1)S(1)} all-to-all(bf16[2,7,16,16,128]{4,3,1,0,2:T(8,128)(2,1)S(1)} %constant_dynamic-update-slice_fusion.16), channel_id=1, replica_groups=mesh['space'=32,'modes'=16] {'modes'}, dimensions={2} | all-to-all | bytes 1835008 | tf_op jit(solution)/shard_map/all_to_all | solution.py:83
  163.3 1.7 fusion.128
  165.0 0.9 slice_bitcast_fusion
  165.8 4.7 %copy.366 = f32[2,4,256,1]{3,2,1,0:T(8,128)S(1)} copy(f32[2,4,256,1]{1,2,0,3:T(8,128)} %get-tuple-element.95) | data formatting | bytes 16384 | tf_op jit(solution)/shard_map/broadcast_in_dim | solution.py:28
  170.6 5.6 %copy.364 = f32[2,4,256,1]{3,2,1,0:T(8,128)} copy(f32[2,4,256,1]{1,2,0,3:T(8,128)} %get-tuple-element.96) | data formatting | bytes 16384 | tf_op jit(solution)/shard_map/broadcast_in_dim | solution.py:27
  176.2 3.7 %fusion.15 = f32[2,4,256,128]{3,2,1,0:T(8,128)} fusion(f32[2,7,256,128]{3,2,1,0:T(8,128)S(1)} %bitcast.421, f32[2,4,256,1]{3,2,1,0:T(8,128)} %copy.364, f32[2,4,256,127]{3,2,1,0:T(8,128)} %get-tuple-element.18, f32[2,4,256,127]{3,2,1,0:T(8,128)} %get-tuple-element.17, f32[2,4,256,1]{3,2,1,0:T(8,128)S(1)} %copy.366), kind=kLoop, calls=%fused_computation.20 | loop fusion | flops 1835008 | bytes 6291456 | tf_op jit(solution)/shard_map/sub | solution.py:90
  179.8 1.6 copy.367
  181.5 0.6 fusion.12
  182.4 0.9 copy.369
  183.3 3.8 %all-to-all-start.3 = ((bf16[2,4,16,16,128]{4,3,1,0,2:T(8,128)(2,1)}), bf16[2,4,16,16,128]{4,3,1,0,2:T(8,128)(2,1)S(1)}, u32[]{:S(2)}, u32[]{:S(2)}) async-start(bf16[2,4,16,16,128]{4,3,1,0,2:T(8,128)(2,1)} %copy.369), calls=%async_computation.3 | async-start | bytes 1048576 | tf_op jit(solution)/shard_map/all_to_all | solution.py:97
  187.1 1.7 fusion.130
  188.8 15.7 %all-to-all-done.3 = bf16[2,4,16,16,128]{4,3,1,0,2:T(8,128)(2,1)S(1)} async-done(((bf16[2,4,16,16,128]{4,3,1,0,2:T(8,128)(2,1)}), bf16[2,4,16,16,128]{4,3,1,0,2:T(8,128)(2,1)S(1)}, u32[]{:S(2)}, u32[]{:S(2)}) %all-to-all-start.3) | async-done | bytes 524320 | tf_op jit(solution)/shard_map/all_to_all | solution.py:97
  204.7 1.4 copy.371
  206.1 2.6 %reshape.97 = f32[2,16,16,512]{3,2,1,0:T(8,128)} reshape(f32[2,4,4,16,4,128]{5,4,3,2,1,0:T(4,128)} %copy.371) | data formatting | bytes 2097152 | tf_op jit(solution)/shard_map/convert_element_type | solution.py:101
  208.7 4.0 %fusion.7 = f32[2,16,16,512]{3,1,2,0:T(8,128)S(1)} fusion(f32[2,16,16,512]{3,2,1,0:T(8,128)} %reshape.97, f32[2,16,16,512]{3,2,1,0:T(8,128)S(1)} %copy-done.2, f32[2,1,16,512]{3,2,1,0:T(8,128)S(1)} %copy-done.21, f32[2,1,16,512]{3,2,1,0:T(8,128)S(1)} %copy-done.19, f32[2,16,512,16]{2,3,1,0:T(8,128)S(1)} %copy-done.4, ...), kind=kOutput, calls=%fused_computation.10 | convolution fusion | flops 54525952 | bytes 7599104 | tf_op jit(solution)/shard_map/ac,fxcy->fxay/dot_general | solution.py:103
  212.8 1.6 copy.372
  (259 shorter events, 27.3 us)
Async XLA Ops:
  0.0 110.2 %copy-start = (f32[1,16,16]{2,1,0:T(8,128)S(1)}, f32[1,16,16]{2,1,0:T(8,128)}, u32[]{:S(2)}) copy-start(f32[1,16,16]{2,1,0:T(8,128)} %param.15) | copy-start | bytes 3076
  1.4 22.3 %collective-permute-start = (f32[2,1,16,512]{3,2,1,0:T(8,128)S(1)}, f32[2,1,16,512]{3,2,1,0:T(8,128)S(1)}, u32[]{:S(2)}, u32[]{:S(2)}) collective-permute-start(f32[2,1,16,512]{3,2,1,0:T(8,128)S(1)} %get-tuple-element.27), channel_id=1, source_target_pairs={{16,0},{32,16},{48,32},{64,48},{80,64},{96,80},{112,96},{128,112},... | collective-permute-start | bytes 196616 | tf_op jit(solution)/shard_map/ppermute | solution.py:15
  5.1 11.1 %collective-permute-start.1 = (f32[2,1,16,512]{3,2,1,0:T(8,128)S(1)}, f32[2,1,16,512]{3,2,1,0:T(8,128)S(1)}, u32[]{:S(2)}, u32[]{:S(2)}) collective-permute-start(f32[2,1,16,512]{3,2,1,0:T(8,128)S(1)} %get-tuple-element.28), channel_id=1, source_target_pairs={{0,16},{16,32},{32,48},{48,64},{64,80},{80,96},{96,112},{112,128},... | collective-permute-start | bytes 196616 | tf_op jit(solution)/shard_map/ppermute | solution.py:14
  16.1 8.2 %copy-start.16 = (f32[2,1,16,512]{3,2,1,0:T(8,128)}, f32[2,1,16,512]{3,2,1,0:T(8,128)S(1)}, u32[]{:S(2)}) copy-start(f32[2,1,16,512]{3,2,1,0:T(8,128)S(1)} %collective-permute-done.1) | copy-start | bytes 196612
  23.7 2.6 %copy-start.14 = (f32[2,1,16,512]{3,2,1,0:T(8,128)}, f32[2,1,16,512]{3,2,1,0:T(8,128)S(1)}, u32[]{:S(2)}) copy-start(f32[2,1,16,512]{3,2,1,0:T(8,128)S(1)} %collective-permute-done) | copy-start | bytes 196612
  24.4 14.6 %copy-start.35 = (s32[3,16,16]{2,1,0:T(8,128)S(1)}, s32[3,16,16]{2,1,0:T(8,128)}, u32[]{:S(2)}) copy-start(s32[3,16,16]{2,1,0:T(8,128)} %param.14) | copy-start | bytes 9220
  24.4 14.6 %copy-start.22 = (f32[2,3,8]{2,0,1:T(2,128)S(1)}, f32[2,3,8]{2,0,1:T(2,128)}, u32[]{:S(2)}) copy-start(f32[2,3,8]{2,0,1:T(2,128)} %param.12) | copy-start | bytes 580
  24.4 15.5 %copy-start.34 = (s32[16,512]{1,0:T(8,128)S(1)}, s32[16,512]{1,0:T(8,128)}, u32[]{:S(2)}) copy-start(s32[16,512]{1,0:T(8,128)} %param.10) | copy-start | bytes 98308
  26.3 40.5 %all-to-all-start = ((bf16[2,7,16,16,128]{4,3,1,0,2:T(8,128)(2,1)}), bf16[2,7,16,16,128]{4,3,1,0,2:T(8,128)(2,1)}, u32[]{:S(2)}, u32[]{:S(2)}) async-start(bf16[2,7,16,16,128]{4,3,1,0,2:T(8,128)(2,1)} %constant_dynamic-update-slice_fusion), calls=%async_computation | async-start | bytes 1835008 | tf_op jit(solution)/shard_map/all_to_all | solution.py:83
  39.9 0.6 copy-start.23
  39.9 0.7 copy-start.25
  39.9 0.7 copy-start.27
  39.9 0.8 copy-start.29
  39.9 0.9 copy-start.31
  39.9 8.2 %copy-start.8 = (f32[16,512]{1,0:T(8,128)}, f32[16,512]{1,0:T(8,128)S(1)}, u32[]{:S(2)}) copy-start(f32[16,512]{1,0:T(8,128)S(1)} %get-tuple-element.102) | copy-start | bytes 98308
  40.0 8.2 %copy-start.10 = (f32[16,512]{1,0:T(8,128)}, f32[16,512]{1,0:T(8,128)S(1)}, u32[]{:S(2)}) copy-start(f32[16,512]{1,0:T(8,128)S(1)} %get-tuple-element.103) | copy-start | bytes 98308
  40.0 8.2 %copy-start.12 = (f32[16,512]{1,0:T(8,128)}, f32[16,512]{1,0:T(8,128)S(1)}, u32[]{:S(2)}) copy-start(f32[16,512]{1,0:T(8,128)S(1)} %get-tuple-element.104) | copy-start | bytes 98308
  48.4 36.5 %copy-start.36 = (f32[2,4,3,128]{3,2,1,0:T(4,128)}, f32[2,4,3,128]{3,2,1,0:T(4,128)S(1)}, u32[]{:S(2)}) copy-start(f32[2,4,3,128]{3,2,1,0:T(4,128)S(1)} %fusion.117) | copy-start | bytes 36868
  83.2 1.7 copy-start.6
  83.2 1.7 copy-start.38
  85.5 5.0 %copy-start.33 = (f32[2,8]{1,0:T(2,128)S(1)}, f32[2,8]{1,0:T(2,128)}, u32[]{:S(2)}) copy-start(f32[2,8]{1,0:T(2,128)} %param.11) | copy-start | bytes 196
  85.5 5.3 %copy-start.9 = (f32[16,512]{1,0:T(8,128)S(1)}, f32[16,512]{1,0:T(8,128)}, u32[]{:S(2)}) copy-start(f32[16,512]{1,0:T(8,128)} %copy-done.8) | copy-start | bytes 98308
  85.5 5.3 %copy-start.11 = (f32[16,512]{1,0:T(8,128)S(1)}, f32[16,512]{1,0:T(8,128)}, u32[]{:S(2)}) copy-start(f32[16,512]{1,0:T(8,128)} %copy-done.10) | copy-start | bytes 98308
  85.6 5.3 %copy-start.13 = (f32[16,512]{1,0:T(8,128)S(1)}, f32[16,512]{1,0:T(8,128)}, u32[]{:S(2)}) copy-start(f32[16,512]{1,0:T(8,128)} %copy-done.12) | copy-start | bytes 98308
  85.6 5.3 %copy-start.24 = (f32[16,512]{1,0:T(8,128)S(1)}, f32[16,512]{1,0:T(8,128)}, u32[]{:S(2)}) copy-start(f32[16,512]{1,0:T(8,128)} %copy-done.23) | copy-start | bytes 98308
  85.6 5.3 %copy-start.26 = (f32[16,512]{1,0:T(8,128)S(1)}, f32[16,512]{1,0:T(8,128)}, u32[]{:S(2)}) copy-start(f32[16,512]{1,0:T(8,128)} %copy-done.25) | copy-start | bytes 98308
  85.6 5.3 %copy-start.28 = (f32[16,512]{1,0:T(8,128)S(1)}, f32[16,512]{1,0:T(8,128)}, u32[]{:S(2)}) copy-start(f32[16,512]{1,0:T(8,128)} %copy-done.27) | copy-start | bytes 98308
  85.6 5.3 %copy-start.30 = (f32[16,512]{1,0:T(8,128)S(1)}, f32[16,512]{1,0:T(8,128)}, u32[]{:S(2)}) copy-start(f32[16,512]{1,0:T(8,128)} %copy-done.29) | copy-start | bytes 98308
  85.6 5.3 %copy-start.32 = (f32[16,512]{1,0:T(8,128)S(1)}, f32[16,512]{1,0:T(8,128)}, u32[]{:S(2)}) copy-start(f32[16,512]{1,0:T(8,128)} %copy-done.31) | copy-start | bytes 98308
  86.8 21.6 %all-to-all-start.1 = ((bf16[2,4,16,16,128]{4,3,1,0,2:T(8,128)(2,1)}), bf16[2,4,16,16,128]{4,3,1,0,2:T(8,128)(2,1)S(1)}, u32[]{:S(2)}, u32[]{:S(2)}) async-start(bf16[2,4,16,16,128]{4,3,1,0,2:T(8,128)(2,1)} %copy.336), calls=%async_computation.1 | async-start | bytes 1048576 | tf_op jit(solution)/shard_map/all_to_all | solution.py:97
  108.3 1.8 copy-start.3
  108.3 1.8 copy-start.15
  108.3 1.8 copy-start.17
  115.2 12.1 %copy-start.1 = (f32[2,16,16,512]{3,2,1,0:T(8,128)}, f32[2,16,16,512]{3,2,1,0:T(8,128)S(1)}, u32[]{:S(2)}) copy-start(f32[2,16,16,512]{3,2,1,0:T(8,128)S(1)} %get-tuple-element.14) | copy-start | bytes 3145732
  116.3 14.3 %collective-permute-start.2 = (f32[2,1,16,512]{3,2,1,0:T(8,128)}, f32[2,1,16,512]{3,2,1,0:T(8,128)S(1)}, u32[]{:S(2)}, u32[]{:S(2)}) collective-permute-start(f32[2,1,16,512]{3,2,1,0:T(8,128)} %get-tuple-element.23), channel_id=1, source_target_pairs={{16,0},{32,16},{48,32},{64,48},{80,64},{96,80},{112,96},{128,112},... | collective-permute-start | bytes 196616 | tf_op jit(solution)/shard_map/ppermute | solution.py:15
  119.7 10.7 %collective-permute-start.3 = (f32[2,1,16,512]{3,2,1,0:T(8,128)}, f32[2,1,16,512]{3,2,1,0:T(8,128)S(1)}, u32[]{:S(2)}, u32[]{:S(2)}) collective-permute-start(f32[2,1,16,512]{3,2,1,0:T(8,128)} %get-tuple-element.24), channel_id=1, source_target_pairs={{0,16},{16,32},{32,48},{48,64},{64,80},{80,96},{96,112},{112,128},... | collective-permute-start | bytes 196616 | tf_op jit(solution)/shard_map/ppermute | solution.py:14
  130.4 0.6 copy-start.20
  130.6 0.6 copy-start.18
  179.8 1.6 copy-start.7
  179.8 1.7 copy-start.37
  179.8 1.7 copy-start.39
  182.1 5.0 %copy-start.2 = (f32[2,16,16,512]{3,2,1,0:T(8,128)S(1)}, f32[2,16,16,512]{3,2,1,0:T(8,128)}, u32[]{:S(2)}) copy-start(f32[2,16,16,512]{3,2,1,0:T(8,128)} %copy-done.1) | copy-start | bytes 3145732
  183.3 21.2 %all-to-all-start.3 = ((bf16[2,4,16,16,128]{4,3,1,0,2:T(8,128)(2,1)}), bf16[2,4,16,16,128]{4,3,1,0,2:T(8,128)(2,1)S(1)}, u32[]{:S(2)}, u32[]{:S(2)}) async-start(bf16[2,4,16,16,128]{4,3,1,0,2:T(8,128)(2,1)} %copy.369), calls=%async_computation.3 | async-start | bytes 1048576 | tf_op jit(solution)/shard_map/all_to_all | solution.py:97
  204.7 4.1 %copy-start.4 = (f32[2,16,512,16]{2,3,1,0:T(8,128)S(1)}, f32[2,16,512,16]{2,3,1,0:T(8,128)}, u32[]{:S(2)}) copy-start(f32[2,16,512,16]{2,3,1,0:T(8,128)} %get-tuple-element.115) | copy-start | bytes 3145732
  204.7 4.1 %copy-start.5 = (bf16[2,16,16,512]{3,2,1,0:T(8,128)(2,1)S(1)}, bf16[2,16,16,512]{3,2,1,0:T(8,128)(2,1)}, u32[]{:S(2)}) copy-start(bf16[2,16,16,512]{3,2,1,0:T(8,128)(2,1)} %param.8) | copy-start | bytes 1572868
  204.7 4.0 %copy-start.19 = (f32[2,1,16,512]{3,2,1,0:T(8,128)S(1)}, f32[2,1,16,512]{3,2,1,0:T(8,128)}, u32[]{:S(2)}) copy-start(f32[2,1,16,512]{3,2,1,0:T(8,128)} %copy-done.18) | copy-start | bytes 196612
  204.7 4.0 %copy-start.21 = (f32[2,1,16,512]{3,2,1,0:T(8,128)S(1)}, f32[2,1,16,512]{3,2,1,0:T(8,128)}, u32[]{:S(2)}) copy-start(f32[2,1,16,512]{3,2,1,0:T(8,128)} %copy-done.20) | copy-start | bytes 196612

commit v2 on v1

v2 whole, which is shorter than its diff:
```python
import jax
import jax.numpy as jnp
from jax import lax
from jax.sharding import PartitionSpec as P

SWEEPS = 2
LANES = 128


def ring_halo(block, axis, dim):
    count = lax.axis_size(axis)
    forward = [(i, (i + 1) % count) for i in range(count)]
    backward = [(target, source) for source, target in forward]
    low = lax.ppermute(lax.slice_in_dim(block, block.shape[dim] - 1, None, axis=dim), axis, forward)
    high = lax.ppermute(lax.slice_in_dim(block, 0, 1, axis=dim), axis, backward)
    return jnp.concatenate([low, block, high], axis=dim)


def lookup(table, region):
    total = jnp.zeros(table.shape[:-1] + region.shape, jnp.float32)
    for which in range(table.shape[-1]):
        total = total + table[..., which, None, None] * (region == which).astype(jnp.float32)
    return total


def laplace_rows(padded, fill_left, fill_right):
    center = padded[:, 1:-1]
    right = jnp.concatenate([center[..., 1:], fill_right[..., None]], -1)
    left = jnp.concatenate([fill_left[..., None], center[..., :-1]], -1)
    return 4.0 * center - padded[:, 2:] - padded[:, :-2] - right - left


def body(rhs, initial, region, base_table, term_table, galerkin, block_mask, block_inverse):
    terms = galerkin.shape[0]
    modes_all = galerkin.shape[1]
    blocks = block_mask.shape[1]
    width = modes_all // blocks
    shaped = galerkin.reshape(terms, blocks, width, blocks, width)
    coupling = (shaped * block_mask[:, :, None, :, None].astype(jnp.bfloat16)).reshape(
        terms, modes_all, modes_all
    )
    coupling = coupling.transpose(1, 0, 2).reshape(modes_all, terms * modes_all)

    fields, modes_dev = rhs.shape[:2]
    rows, cols = region.shape
    devs = lax.axis_size("modes")
    spaces = lax.axis_size("space")
    col_chunks = cols // LANES
    row_chunks = devs // col_chunks
    rows_c = rows // row_chunks
    me = lax.axis_index("modes")
    my_r = me // col_chunks
    my_c = me % col_chunks

    every = lax.all_gather(block_inverse, "modes", tiled=True)
    eye = jnp.eye(blocks, dtype=jnp.float32)
    dense_inv = (every[:, :, None, :] * eye[:, None, :, None]).reshape(modes_all, modes_all)

    base = lax.dynamic_slice(
        lookup(base_table, region), (0, my_r * rows_c, my_c * LANES), (fields, rows_c, LANES)
    )[:, :, None, :]
    coef = lax.dynamic_slice(
        lookup(term_table, region),
        (0, 0, my_r * rows_c, my_c * LANES),
        (fields, terms, rows_c, LANES),
    )
    coef = coef.transpose(0, 2, 1, 3)[:, :, :, None, :]
    inverse_base = 1.0 / (4.0 * base)

    rhs_p = rhs.reshape(fields, modes_dev, row_chunks, rows_c, col_chunks, LANES)
    rhs_p = rhs_p.transpose(0, 3, 2, 4, 1, 5).reshape(fields, rows_c, devs, modes_dev, LANES)
    rhs_c = lax.all_to_all(rhs_p, "modes", split_axis=2, concat_axis=3, tiled=True)[:, :, 0]
    rhs_c = rhs_c.astype(jnp.float32)

    init_x = ring_halo(initial.transpose(0, 2, 1, 3), "space", 1)
    zero_col = jnp.zeros((fields, rows_c, modes_dev), init_x.dtype)
    pieces = []
    for r in range(row_chunks):
        for c in range(col_chunks):
            main = init_x[:, r * rows_c : r * rows_c + rows_c + 2, :, c * LANES : (c + 1) * LANES]
            inner = init_x[:, r * rows_c + 1 : r * rows_c + rows_c + 1]
            hl = inner[..., c * LANES - 1] if c > 0 else zero_col
            hr = inner[..., (c + 1) * LANES] if c < col_chunks - 1 else zero_col
            side = jnp.concatenate([hl, hr], axis=1).transpose(0, 2, 1)
            side = jnp.pad(side, ((0, 0), (0, 0), (0, LANES - 2 * rows_c)))[:, None]
            pieces.append(jnp.concatenate([main, side], axis=1))
    stacked = jnp.stack(pieces, axis=2)
    got = lax.all_to_all(stacked, "modes", split_axis=2, concat_axis=3, tiled=True)[:, :, 0]
    got = got.astype(jnp.float32)
    side = got[:, rows_c + 2]
    fill_l = side[..., :rows_c].transpose(0, 2, 1)
    fill_r = side[..., rows_c : 2 * rows_c].transpose(0, 2, 1)
    padded = got[:, : rows_c + 2]
    u_field = padded[:, 1:-1]

    flat = ("space", "modes")
    total_rc = spaces * row_chunks

    def dev_of(g, c):
        s, r = divmod(g % total_rc, row_chunks)
        return s * devs + r * col_chunks + c

    down = [(dev_of(g, c), dev_of(g + 1, c)) for g in range(total_rc) for c in range(col_chunks)]
    up = [(b, a) for a, b in down]
    rightward = [
        (s * devs + r * col_chunks + c, s * devs + r * col_chunks + c + 1)
        for s in range(spaces)
        for r in range(row_chunks)
        for c in range(col_chunks - 1)
    ]
    leftward = [(b, a) for a, b in rightward]

    for sweep in range(SWEEPS):
        if sweep > 0:
            low = lax.ppermute(u_field[:, -1:], flat, down)
            high = lax.ppermute(u_field[:, :1], flat, up)
            fill_l = lax.ppermute(u_field[..., -1], flat, rightward)
            fill_r = lax.ppermute(u_field[..., 0], flat, leftward)
            padded = jnp.concatenate([low, u_field, high], axis=1)
        lap = laplace_rows(padded, fill_l, fill_r)
        local = base * lap
        if sweep > 0:
            lap_r = laplace_rows(
                padded.astype(jnp.bfloat16).astype(jnp.float32),
                fill_l.astype(jnp.bfloat16).astype(jnp.float32),
                fill_r.astype(jnp.bfloat16).astype(jnp.float32),
            )
        else:
            lap_r = lap
        tiles = (coef * lap_r[:, :, None]).astype(jnp.bfloat16)
        tiles = tiles.reshape(fields, rows_c, terms * modes_all, LANES)
        coupled = jnp.einsum(
            "ic,fxcy->fxiy", coupling, tiles, preferred_element_type=jnp.float32
        ).astype(jnp.bfloat16)
        resid = rhs_c - local - coupled.astype(jnp.float32)
        scaled = resid * inverse_base
        update = jnp.einsum("ij,fxjy->fxiy", dense_inv, scaled, precision=lax.Precision.HIGHEST)
        u_field = u_field + 0.6 * update

    out = u_field.reshape(fields, rows_c, devs, modes_dev, LANES)
    back = lax.all_to_all(out, "modes", split_axis=2, concat_axis=2, tiled=True)
    back = back.reshape(fields, rows_c, row_chunks, col_chunks, modes_dev, LANES)
    return back.transpose(0, 4, 2, 1, 3, 5).reshape(fields, modes_dev, rows, cols)


def solution(mesh):
    in_specs = (
        P(None, "modes", "space", None),
        P(None, "modes", "space", None),
        P("space", None),
        P(),
        P(),
        P(),
        P(),
        P("modes", None, None),
    )
    out_specs = P(None, "modes", "space", None)
    return jax.shard_map(body, mesh=mesh, in_specs=in_specs, out_specs=out_specs, check_vma=False)
```

time: 217 us -> 191 us (0.88)
  blocking collectives: 31.8 us -> 83 us
  waiting for transfers between devices: 49.8 us -> 5.49 us
  local copies, waits for them, and re-layouts: 69.3 us -> 37.4 us
  starting transfers between devices: 31 us -> 39.2 us
  matrix products: 10.4 us -> 4.08 us
  other arithmetic: 21.1 us -> 17.5 us
    all_gather x0 -> x1, blocking collectives: none -> 43.1 us  [body(): every = lax.all_gather(block_inverse, 'modes', tiled=True)]
    all_to_all x2 -> x1, waiting for transfers between devices: 31.3 us -> 4.16 us  [body(): lax.all_to_all(rhs_p, 'modes', split_axis=2, concat_axis=3, tiled=True)]
    broadcast_in_dim x6, local copies, waits for them, and re-layouts: 20.6 us -> 0.05 us  [the longest x3 0.03 us: laplace_rows(): right = jnp.concatenate([center[..., 1:], fill_right[..., None]], -1)]
    all_to_all x1, waiting for transfers between devices: 18.4 us -> 0.01 us  [body(): lax.all_to_all(stacked, 'modes', split_axis=2, concat_axis=3, tiled=True)]
    squeeze x50 -> x0, local copies, waits for them, and re-layouts: 15.1 us -> none  [the longest x24 7.54 us: body(): hr = inner[..., (c + 1) * LANES] if c < col_chunks - 1 else zero_col]
    ppermute x0 -> x4, starting transfers between devices: none -> 14.3 us  [the longest x1 6.05 us: body(): fill_l = lax.ppermute(u_field[..., -1], flat, rightward)]
    unnamed x80 -> x41, local copies, waits for them, and re-layouts: 1.18 us -> 12.1 us
    all_to_all x1, blocking collectives: 31.8 us -> 39.9 us  [body(): back = lax.all_to_all(out, 'modes', split_axis=2, concat_axis=2, tiled=True)]
  transfers between devices with their start and end apart: 7 -> 8, of which waited for: 3 -> 2; matrix products, arithmetic and copies ran while one was open for 18% -> 17% of each run, Pallas kernels for 0% -> 0%
where the time goes in v2:
time: 191 us; the launch traced here: 187 us
  blocking collectives  83 us (43%)
  starting transfers between devices  39.2 us (21%)
  local copies, waits for them, and re-layouts  37.4 us (20%)
  other arithmetic  17.5 us (9%)
  waiting for transfers between devices  5.49 us (3%)
  matrix products  4.08 us (2%)
    all_gather x1, blocking collectives, body(): every = lax.all_gather(block_inverse, 'modes', tiled=True)  43.1 us
    all_to_all x1, blocking collectives, body(): back = lax.all_to_all(out, 'modes', split_axis=2, concat_axis=2, tiled=True)  39.9 us
    all_to_all x1, starting transfers between devices, body(): lax.all_to_all(rhs_p, 'modes', split_axis=2, concat_axis=3, tiled=True)  13 us
    unnamed x41, local copies, waits for them, and re-layouts  12.1 us
    unnamed x15, other arithmetic  9.46 us
    ppermute x1, starting transfers between devices, body(): fill_l = lax.ppermute(u_field[..., -1], flat, rightward)  6.05 us
    slice x10, local copies, waits for them, and re-layouts, lookup(): table[..., which, None, None] * (region == which).astype(jnp.float32)  5.71 us
    all_to_all x1, starting transfers between devices, body(): lax.all_to_all(stacked, 'modes', split_axis=2, concat_axis=3, tiled=True)  5.51 us
  transfers between devices with their start and end apart: 8, of which 2 were waited for; matrix products, arithmetic and copies ran while one was open for 17% of the time, Pallas kernels for 0%

profile of v2, /device:TPU:56, one launch (start us, length us, event | category | flops | bytes accessed | tf_op | source)
XLA Modules:
  0.0 187.5 jit_solution(6587479706086710269)
XLA Ops:
  0.0 1.3 copy.243
  1.3 1.9 %collective-permute-start = (bf16[2,1,16,512]{3,2,1,0:T(8,128)(2,1)S(1)}, bf16[2,1,16,512]{3,2,1,0:T(8,128)(2,1)S(1)}, u32[]{:S(2)}, u32[]{:S(2)}) collective-permute-start(bf16[2,1,16,512]{3,2,1,0:T(8,128)(2,1)S(1)} %get-tuple-element.53), channel_id=1, source_target_pairs={{0,16},{16,32},{32,48},{48,64},{64,80},{80,96},{96,112},{112,128},... | collective-permute-start | bytes 98312 | tf_op jit(solution)/shard_map/ppermute | solution.py:14
  3.3 4.5 %collective-permute-start.1 = (bf16[2,1,16,512]{3,2,1,0:T(8,128)(2,1)S(1)}, bf16[2,1,16,512]{3,2,1,0:T(8,128)(2,1)S(1)}, u32[]{:S(2)}, u32[]{:S(2)}) collective-permute-start(bf16[2,1,16,512]{3,2,1,0:T(8,128)(2,1)S(1)} %get-tuple-element.52), channel_id=1, source_target_pairs={{16,0},{32,16},{48,32},{64,48},{80,64},{96,80},{112,96},{128,112},... | collective-permute-start | bytes 98312 | tf_op jit(solution)/shard_map/ppermute | solution.py:15
  7.8 1.2 reshape.87
  9.0 1.1 copy.203
  10.1 13.0 %all-to-all-start.1 = ((bf16[2,4,16,16,128]{4,3,1,0,2:T(8,128)(2,1)}), bf16[2,4,16,16,128]{4,3,1,0,2:T(8,128)(2,1)S(1)}, u32[]{:S(2)}, u32[]{:S(2)}) async-start(bf16[2,4,16,16,128]{4,3,1,0,2:T(8,128)(2,1)} %bitcast.51), calls=%async_computation.1 | async-start | bytes 1048576 | tf_op jit(solution)/shard_map/all_to_all | solution.py:72
  24.5 0.6 compare_convert_fusion.4
  26.5 0.7 fusion.44
  34.1 0.6 fusion.68
  36.6 4.2 %all-to-all-done.1 = bf16[2,4,16,16,128]{4,3,1,0,2:T(8,128)(2,1)S(1)} async-done(((bf16[2,4,16,16,128]{4,3,1,0,2:T(8,128)(2,1)}), bf16[2,4,16,16,128]{4,3,1,0,2:T(8,128)(2,1)S(1)}, u32[]{:S(2)}, u32[]{:S(2)}) %all-to-all-start.1) | async-done | bytes 524320 | tf_op jit(solution)/shard_map/all_to_all | solution.py:72
  40.8 5.5 %all-to-all-start = ((bf16[2,7,16,16,128]{4,3,1,0,2:T(8,128)(2,1)}), bf16[2,7,16,16,128]{4,3,1,0,2:T(8,128)(2,1)}, u32[]{:S(2)}, u32[]{:S(2)}) async-start(bf16[2,7,16,16,128]{4,3,1,0,2:T(8,128)(2,1)} %fusion.59), calls=%async_computation | async-start | bytes 1835008 | tf_op jit(solution)/shard_map/all_to_all | solution.py:88
  46.4 0.7 copy.213
  47.1 0.7 copy.212
  47.8 0.7 copy.214
  48.5 0.7 copy.219
  49.3 0.7 copy.218
  50.0 0.7 copy.217
  50.8 0.7 copy.216
  51.4 0.6 dynamic-slice
  52.1 0.7 copy.215
  53.2 3.0 %mul.429 = bf16[3,256,256]{2,1,0:T(8,128)(2,1)S(1)} reshape(bf16[3,16,16,16,16]{4,3,2,1,0:T(8,128)(2,1)S(1)} %mul.428) | data formatting | bytes 786432 | tf_op jit(solution)/shard_map/mul | solution.py:39
  56.3 43.1 %all_gather.3 = f32[16,16,16]{2,1,0:T(8,128)S(1)} all-gather(f32[1,16,16]{2,1,0:T(8,128)} %param.15), channel_id=1, replica_groups=mesh['space'=32,'modes'=16] {'modes'}, dimensions={0}, use_global_device_ids=true | all-gather | bytes 17408 | tf_op jit(solution)/shard_map/all_gather | solution.py:55
  99.6 0.9 reshape.98
  101.0 0.7 multiply_divide_fusion
  101.7 1.0 multiply_add_fusion
  102.7 1.4 fusion.82
  104.2 1.3 copy.211
  105.5 1.4 copy.201
  107.2 1.9 %fusion.90 = (f32[2,4,256,128]{3,2,1,0:T(8,128)S(1)}, f32[2,4,256,128]{3,2,1,0:T(8,128)}, f32[2,4,256,128]{3,2,1,0:T(8,128)}) fusion(f32[2,7,256,128]{3,2,1,0:T(8,128)S(1)} %bitcast_convert_fusion), kind=kLoop, calls=%fused_computation.203 | loop fusion | bytes 6291456 | tf_op jit(solution)/shard_map/slice | solution.py:30
  109.1 1.7 fusion.91
  110.8 1.6 copy.232
  112.6 2.6 %copy.235 = f32[2,4,256,127]{2,3,1,0:T(8,128)} copy(f32[2,4,256,127]{3,2,1,0:T(8,128)} %get-tuple-element.43) | data formatting | bytes 2080768
  115.2 2.6 %copy.237 = f32[2,4,256,127]{2,3,1,0:T(8,128)} copy(f32[2,4,256,127]{3,2,1,0:T(8,128)} %get-tuple-element.42) | data formatting | bytes 2080768
  117.7 2.5 %copy.234 = f32[2,4,256,128]{2,3,1,0:T(8,128)} copy(f32[2,4,256,128]{3,2,1,0:T(8,128)} %get-tuple-element.40) | data formatting | bytes 2097152
  120.3 1.3 copy.233
  121.6 2.6 %fusion.30 = f32[2,4,256,128]{2,3,1,0:T(8,128)S(1)} fusion(f32[2,4,256,1]{2,3,1,0:T(1,128)S(1)} %copy.209, f32[2,4,256,127]{2,3,1,0:T(8,128)} %copy.235, f32[2,4,256,127]{2,3,1,0:T(8,128)} %copy.237, f32[2,4,256,1]{2,3,1,0:T(1,128)S(1)} %broadcast_in_dim.113, f32[2,4,256,128]{2,3,1,0:T(8,128)} %copy.234, f32[2,4,256,128]{2,3,1,0:T(8,128)} %copy.233, ...), kind=kLoop, calls=%fused_computation.40 | loop fusion | flops 1835008 | bytes 6291456 | tf_op jit(solution)/shard_map/sub | solution.py:30
  124.3 0.9 fusion.16
  125.2 1.1 fusion.99
  126.5 1.5 collective-permute-start.4
  128.0 1.9 %collective-permute-start.2 = (f32[2,1,256,128]{2,3,1,0:T(8,128)S(1)}, f32[2,1,256,128]{2,3,1,0:T(8,128)S(1)}, u32[]{:S(2)}, u32[]{:S(2)}) collective-permute-start(f32[2,1,256,128]{2,3,1,0:T(8,128)S(1)} %get-tuple-element.51), channel_id=1, source_target_pairs={{4,0},{5,1},{6,2},{7,3},{8,4},{9,5},{10,6},{11,7},{12,8},{13,9},{1... | collective-permute-start | bytes 786440 | tf_op jit(solution)/shard_map/ppermute | solution.py:116
  129.9 4.8 %collective-permute-start.3 = (f32[2,1,256,128]{2,3,1,0:T(8,128)S(1)}, f32[2,1,256,128]{2,3,1,0:T(8,128)S(1)}, u32[]{:S(2)}, u32[]{:S(2)}) collective-permute-start(f32[2,1,256,128]{2,3,1,0:T(8,128)S(1)} %get-tuple-element.50), channel_id=1, source_target_pairs={{0,4},{1,5},{2,6},{3,7},{4,8},{5,9},{6,10},{7,11},{8,12},{9,13},{1... | collective-permute-start | bytes 786440 | tf_op jit(solution)/shard_map/ppermute | solution.py:115
  134.7 6.1 %collective-permute-start.5 = (f32[2,4,256]{2,1,0:T(4,128)S(1)}, f32[2,4,256]{2,1,0:T(4,128)S(1)}, u32[]{:S(2)}, u32[]{:S(2)}) collective-permute-start(f32[2,4,256]{2,1,0:T(4,128)S(1)} %bitcast.257), channel_id=1, source_target_pairs={{0,1},{1,2},{2,3},{4,5},{5,6},{6,7},{8,9},{9,10},{10,11},{12,13},{... | collective-permute-start | bytes 24584 | tf_op jit(solution)/shard_map/ppermute | solution.py:117
  140.8 1.3 collective-permute-done.5
  142.9 1.1 fusion.21
  144.0 1.0 fusion.9
  145.5 39.9 %all_to_all.23 = f32[2,4,16,16,128]{4,3,1,0,2:T(8,128)S(1)} all-to-all(f32[2,4,16,16,128]{4,3,1,0,2:T(8,128)S(1)} %copy.226), channel_id=1, replica_groups=mesh['space'=32,'modes'=16] {'modes'}, dimensions={2} | all-to-all | bytes 2097152 | tf_op jit(solution)/shard_map/all_to_all | solution.py:141
  185.4 0.7 copy.227
  186.1 1.4 reshape.91
  (135 shorter events, 14.7 us)
Async XLA Ops:
  1.3 25.2 %collective-permute-start = (bf16[2,1,16,512]{3,2,1,0:T(8,128)(2,1)S(1)}, bf16[2,1,16,512]{3,2,1,0:T(8,128)(2,1)S(1)}, u32[]{:S(2)}, u32[]{:S(2)}) collective-permute-start(bf16[2,1,16,512]{3,2,1,0:T(8,128)(2,1)S(1)} %get-tuple-element.53), channel_id=1, source_target_pairs={{0,16},{16,32},{32,48},{48,64},{64,80},{80,96},{96,112},{112,128},... | collective-permute-start | bytes 98312 | tf_op jit(solution)/shard_map/ppermute | solution.py:14
  3.3 30.8 %collective-permute-start.1 = (bf16[2,1,16,512]{3,2,1,0:T(8,128)(2,1)S(1)}, bf16[2,1,16,512]{3,2,1,0:T(8,128)(2,1)S(1)}, u32[]{:S(2)}, u32[]{:S(2)}) collective-permute-start(bf16[2,1,16,512]{3,2,1,0:T(8,128)(2,1)S(1)} %get-tuple-element.52), channel_id=1, source_target_pairs={{16,0},{32,16},{48,32},{64,48},{80,64},{96,80},{112,96},{128,112},... | collective-permute-start | bytes 98312 | tf_op jit(solution)/shard_map/ppermute | solution.py:15
  10.1 14.3 %copy-start.9 = (s32[16,512]{1,0:T(8,128)S(1)}, s32[16,512]{1,0:T(8,128)}, u32[]{:S(2)}) copy-start(s32[16,512]{1,0:T(8,128)} %param.10) | copy-start | bytes 98308
  10.1 30.7 %all-to-all-start.1 = ((bf16[2,4,16,16,128]{4,3,1,0,2:T(8,128)(2,1)}), bf16[2,4,16,16,128]{4,3,1,0,2:T(8,128)(2,1)S(1)}, u32[]{:S(2)}, u32[]{:S(2)}) async-start(bf16[2,4,16,16,128]{4,3,1,0,2:T(8,128)(2,1)} %bitcast.51), calls=%async_computation.1 | async-start | bytes 1048576 | tf_op jit(solution)/shard_map/all_to_all | solution.py:72
  34.7 11.6 %copy-start.7 = (f32[2,3,8]{2,0,1:T(2,128)S(1)}, f32[2,3,8]{2,0,1:T(2,128)}, u32[]{:S(2)}) copy-start(f32[2,3,8]{2,0,1:T(2,128)} %param.12) | copy-start | bytes 580
  34.7 18.0 %copy-start.10 = (s32[3,16,16]{2,1,0:T(8,128)S(1)}, s32[3,16,16]{2,1,0:T(8,128)}, u32[]{:S(2)}) copy-start(s32[3,16,16]{2,1,0:T(8,128)} %param.14) | copy-start | bytes 9220
  40.8 11.9 %copy-start.1 = (bf16[2,4,16,16,128]{4,3,1,0,2:T(8,128)(2,1)}, bf16[2,4,16,16,128]{4,3,1,0,2:T(8,128)(2,1)S(1)}, u32[]{:S(2)}) copy-start(bf16[2,4,16,16,128]{4,3,1,0,2:T(8,128)(2,1)S(1)} %all-to-all-done.1) | copy-start | bytes 1572868
  40.8 64.7 %all-to-all-start = ((bf16[2,7,16,16,128]{4,3,1,0,2:T(8,128)(2,1)}), bf16[2,7,16,16,128]{4,3,1,0,2:T(8,128)(2,1)}, u32[]{:S(2)}, u32[]{:S(2)}) async-start(bf16[2,7,16,16,128]{4,3,1,0,2:T(8,128)(2,1)} %fusion.59), calls=%async_computation | async-start | bytes 1835008 | tf_op jit(solution)/shard_map/all_to_all | solution.py:88
  99.4 1.2 copy-start.8
  99.4 1.5 copy-start.4
  99.4 1.5 copy-start.5
  99.4 1.5 copy-start.6
  99.6 1.4 copy-start.11
  99.6 4.4 %copy-start.2 = (bf16[2,4,16,16,128]{4,3,1,0,2:T(8,128)(2,1)S(1)}, bf16[2,4,16,16,128]{4,3,1,0,2:T(8,128)(2,1)}, u32[]{:S(2)}) copy-start(bf16[2,4,16,16,128]{4,3,1,0,2:T(8,128)(2,1)} %copy-done.1) | copy-start | bytes 1572868
  107.2 1.9 %copy-start = (f32[2,7,256,128]{3,2,1,0:T(8,128)}, f32[2,7,256,128]{3,2,1,0:T(8,128)S(1)}, u32[]{:S(2)}) copy-start(f32[2,7,256,128]{3,2,1,0:T(8,128)S(1)} %bitcast_convert_fusion) | copy-start | bytes 5505028
  110.8 1.6 slice-start
  121.6 2.7 %copy-start.3 = (f32[2,4,256,128]{2,3,1,0:T(8,128)S(1)}, f32[2,4,256,128]{2,3,1,0:T(8,128)}, u32[]{:S(2)}) copy-start(f32[2,4,256,128]{2,3,1,0:T(8,128)} %copy.211) | copy-start | bytes 3145732
  121.6 2.7 %copy-start.12 = (f32[2,4,3,128]{3,2,1,0:T(4,128)S(1)}, f32[2,4,3,128]{3,2,1,0:T(4,128)}, u32[]{:S(2)}) copy-start(f32[2,4,3,128]{3,2,1,0:T(4,128)} %fusion.82) | copy-start | bytes 36868
  121.6 2.7 %copy-start.13 = (f32[2,4,128]{2,1,0:T(4,128)S(1)}, f32[2,4,128]{2,1,0:T(4,128)}, u32[]{:S(2)}) copy-start(f32[2,4,128]{2,1,0:T(4,128)} %get-tuple-element.37) | copy-start | bytes 12292
  121.6 2.7 %copy-start.14 = (f32[2,4,128]{2,1,0:T(4,128)S(1)}, f32[2,4,128]{2,1,0:T(4,128)}, u32[]{:S(2)}) copy-start(f32[2,4,128]{2,1,0:T(4,128)} %get-tuple-element.38) | copy-start | bytes 12292
  121.6 2.7 %copy-start.15 = (bf16[3,256,256]{2,1,0:T(8,128)(2,1)S(1)}, bf16[3,256,256]{2,1,0:T(8,128)(2,1)}, u32[]{:S(2)}) copy-start(bf16[3,256,256]{2,1,0:T(8,128)(2,1)} %param.13) | copy-start | bytes 1179652
  126.5 14.4 %collective-permute-start.4 = (f32[2,4,256]{2,1,0:T(4,128)S(1)}, f32[2,4,256]{2,1,0:T(4,128)S(1)}, u32[]{:S(2)}, u32[]{:S(2)}) collective-permute-start(f32[2,4,256]{2,1,0:T(4,128)S(1)} %bitcast.256), channel_id=1, source_target_pairs={{1,0},{2,1},{3,2},{5,4},{6,5},{7,6},{9,8},{10,9},{11,10},{13,12},{... | collective-permute-start | bytes 24584 | tf_op jit(solution)/shard_map/ppermute | solution.py:118
  128.0 14.2 %collective-permute-start.2 = (f32[2,1,256,128]{2,3,1,0:T(8,128)S(1)}, f32[2,1,256,128]{2,3,1,0:T(8,128)S(1)}, u32[]{:S(2)}, u32[]{:S(2)}) collective-permute-start(f32[2,1,256,128]{2,3,1,0:T(8,128)S(1)} %get-tuple-element.51), channel_id=1, source_target_pairs={{4,0},{5,1},{6,2},{7,3},{8,4},{9,5},{10,6},{11,7},{12,8},{13,9},{1... | collective-permute-start | bytes 786440 | tf_op jit(solution)/shard_map/ppermute | solution.py:116
  129.9 12.3 %collective-permute-start.3 = (f32[2,1,256,128]{2,3,1,0:T(8,128)S(1)}, f32[2,1,256,128]{2,3,1,0:T(8,128)S(1)}, u32[]{:S(2)}, u32[]{:S(2)}) collective-permute-start(f32[2,1,256,128]{2,3,1,0:T(8,128)S(1)} %get-tuple-element.50), channel_id=1, source_target_pairs={{0,4},{1,5},{2,6},{3,7},{4,8},{5,9},{6,10},{7,11},{8,12},{9,13},{1... | collective-permute-start | bytes 786440 | tf_op jit(solution)/shard_map/ppermute | solution.py:115
  134.7 7.4 %collective-permute-start.5 = (f32[2,4,256]{2,1,0:T(4,128)S(1)}, f32[2,4,256]{2,1,0:T(4,128)S(1)}, u32[]{:S(2)}, u32[]{:S(2)}) collective-permute-start(f32[2,4,256]{2,1,0:T(4,128)S(1)} %bitcast.257), channel_id=1, source_target_pairs={{0,1},{1,2},{2,3},{4,5},{5,6},{6,7},{8,9},{9,10},{10,11},{12,13},{... | collective-permute-start | bytes 24584 | tf_op jit(solution)/shard_map/ppermute | solution.py:117

commit v3 on v2

v3 whole, which is shorter than its diff:
```python
import jax
import jax.numpy as jnp
from jax import lax
from jax.sharding import PartitionSpec as P

SWEEPS = 2
LANES = 128


def ring_halo(block, axis, dim):
    count = lax.axis_size(axis)
    forward = [(i, (i + 1) % count) for i in range(count)]
    backward = [(target, source) for source, target in forward]
    low = lax.ppermute(lax.slice_in_dim(block, block.shape[dim] - 1, None, axis=dim), axis, forward)
    high = lax.ppermute(lax.slice_in_dim(block, 0, 1, axis=dim), axis, backward)
    return jnp.concatenate([low, block, high], axis=dim)


def lookup(table, region):
    total = jnp.zeros(table.shape[:-1] + region.shape, jnp.float32)
    for which in range(table.shape[-1]):
        total = total + table[..., which, None, None] * (region == which).astype(jnp.float32)
    return total


def laplace_rows(padded, fill_left, fill_right):
    center = padded[1:-1]
    right = jnp.concatenate([center[..., 1:], fill_right[..., None]], -1)
    left = jnp.concatenate([fill_left[..., None], center[..., :-1]], -1)
    return 4.0 * center - padded[2:] - padded[:-2] - right - left


def body(rhs, initial, region, base_table, term_table, galerkin, block_mask, block_inverse):
    terms = galerkin.shape[0]
    modes_all = galerkin.shape[1]
    blocks = block_mask.shape[1]
    width = modes_all // blocks
    shaped = galerkin.reshape(terms, blocks, width, blocks, width)
    coupling = (shaped * block_mask[:, :, None, :, None].astype(jnp.bfloat16)).reshape(
        terms, modes_all, modes_all
    )
    coupling = coupling.transpose(1, 0, 2).reshape(modes_all, terms * modes_all)

    fields, modes_dev = rhs.shape[:2]
    rows, cols = region.shape
    devs = lax.axis_size("modes")
    spaces = lax.axis_size("space")
    col_chunks = cols // LANES
    row_chunks = devs // col_chunks
    rows_c = rows // row_chunks
    me = lax.axis_index("modes")
    my_r = me // col_chunks
    my_c = me % col_chunks

    every = lax.all_to_all(
        jnp.broadcast_to(block_inverse, (devs,) + block_inverse.shape[1:]),
        "modes", split_axis=0, concat_axis=0, tiled=True,
    )
    eye = jnp.eye(blocks, dtype=jnp.float32)
    dense_inv = (every[:, :, None, :] * eye[:, None, :, None]).reshape(modes_all, modes_all)

    base = lax.dynamic_slice(
        lookup(base_table, region), (0, my_r * rows_c, my_c * LANES), (fields, rows_c, LANES)
    )[:, :, None, :]
    coef = lax.dynamic_slice(
        lookup(term_table, region),
        (0, 0, my_r * rows_c, my_c * LANES),
        (fields, terms, rows_c, LANES),
    )
    coef = coef.transpose(0, 2, 1, 3)[:, :, :, None, :]
    inverse_base = 1.0 / (4.0 * base)

    init_x = ring_halo(initial.transpose(0, 2, 1, 3), "space", 1)

    flat = ("space", "modes")
    total_rc = spaces * row_chunks

    def dev_of(g, c):
        s, r = divmod(g % total_rc, row_chunks)
        return s * devs + r * col_chunks + c

    down = [(dev_of(g, c), dev_of(g + 1, c)) for g in range(total_rc) for c in range(col_chunks)]
    up = [(b, a) for a, b in down]
    rightward = [
        (s * devs + r * col_chunks + c, s * devs + r * col_chunks + c + 1)
        for s in range(spaces)
        for r in range(row_chunks)
        for c in range(col_chunks - 1)
    ]
    leftward = [(b, a) for a, b in rightward]

    def pack(init_f, rhs_f):
        top = init_f[0 : rows : rows_c]
        mid = init_f[1 : rows + 1].reshape(row_chunks, rows_c, modes_dev, cols)
        bot = init_f[rows_c + 1 : rows + 2 : rows_c]
        main = jnp.concatenate([top[:, None], mid, bot[:, None]], axis=1)
        main = main.reshape(row_chunks, rows_c + 2, modes_dev, col_chunks, LANES)
        inner = init_f[1 : rows + 1]
        hl = jnp.pad(inner[..., LANES - 1 : cols - 1 : LANES], ((0, 0), (0, 0), (1, 0)))
        hr = jnp.pad(inner[..., LANES : cols : LANES], ((0, 0), (0, 0), (0, 1)))
        sides = []
        for h in (hl, hr):
            sides.append(h.reshape(row_chunks, rows_c, modes_dev, col_chunks).transpose(0, 2, 3, 1))
        side = jnp.concatenate(sides, axis=-1)
        side = jnp.pad(side, ((0, 0), (0, 0), (0, 0), (0, LANES - 2 * rows_c)))[:, None]
        rp = rhs_f.reshape(modes_dev, row_chunks, rows_c, col_chunks, LANES).transpose(1, 2, 0, 3, 4)
        full = jnp.concatenate([main, side, rp], axis=1)
        full = full.transpose(0, 3, 1, 2, 4).reshape(devs, -1, modes_dev, LANES)
        return lax.all_to_all(full, "modes", split_axis=0, concat_axis=2, tiled=True)[0]

    outs = []
    for f in range(fields):
        got = pack(init_x[f], rhs[f])
        padded = got[: rows_c + 2].astype(jnp.float32)
        side = got[rows_c + 2].astype(jnp.float32)
        fill_l = side[:, :rows_c].T
        fill_r = side[:, rows_c : 2 * rows_c].T
        rhs_c = got[rows_c + 3 :].astype(jnp.float32)
        u_field = padded[1:-1]
        for sweep in range(SWEEPS):
            if sweep > 0:
                low = lax.ppermute(u_field[-1:], flat, down)
                high = lax.ppermute(u_field[:1], flat, up)
                fill_l = lax.ppermute(u_field[..., -1], flat, rightward)
                fill_r = lax.ppermute(u_field[..., 0], flat, leftward)
                padded = jnp.concatenate([low, u_field, high], axis=0)
            lap = laplace_rows(padded, fill_l, fill_r)
            local = base[f] * lap
            if sweep > 0:
                lap_r = laplace_rows(
                    padded.astype(jnp.bfloat16).astype(jnp.float32),
                    fill_l.astype(jnp.bfloat16).astype(jnp.float32),
                    fill_r.astype(jnp.bfloat16).astype(jnp.float32),
                )
            else:
                lap_r = lap
            tiles = (coef[f] * lap_r[:, None]).astype(jnp.bfloat16)
            tiles = tiles.reshape(rows_c, terms * modes_all, LANES)
            coupled = jnp.einsum(
                "ic,xcy->xiy", coupling, tiles, preferred_element_type=jnp.float32
            ).astype(jnp.bfloat16)
            resid = rhs_c - local - coupled.astype(jnp.float32)
            scaled = resid * inverse_base[f]
            update = jnp.einsum("ij,xjy->xiy", dense_inv, scaled, precision=lax.Precision.HIGHEST)
            u_field = u_field + 0.6 * update
        out = u_field.reshape(rows_c, devs, modes_dev, LANES)
        back = lax.all_to_all(out, "modes", split_axis=1, concat_axis=1, tiled=True)
        back = back.reshape(rows_c, row_chunks, col_chunks, modes_dev, LANES)
        outs.append(back.transpose(3, 1, 0, 2, 4).reshape(modes_dev, rows, cols))
    return jnp.stack(outs)


def solution(mesh):
    in_specs = (
        P(None, "modes", "space", None),
        P(None, "modes", "space", None),
        P("space", None),
        P(),
        P(),
        P(),
        P(),
        P("modes", None, None),
    )
    out_specs = P(None, "modes", "space", None)
    return jax.shard_map(body, mesh=mesh, in_specs=in_specs, out_specs=out_specs, check_vma=False)
```

time: 191 us -> 213 us (1.12)
  the two profiles are of different devices: /device:TPU:56 before, /device:TPU:26 now
where the time goes in v3:
time: 213 us; the launch traced here: 211 us
  starting transfers between devices  78.4 us (37%)
  local copies, waits for them, and re-layouts  73 us (34%)
  waiting for transfers between devices  39.7 us (19%)
  other arithmetic  11.5 us (5%)
  matrix products  7.44 us (3%)
    all_to_all x2, waiting for transfers between devices, body(): back = lax.all_to_all(out, 'modes', split_axis=1, concat_axis=1, tiled=True)  29.6 us
    all_to_all x2, starting transfers between devices, pack(): lax.all_to_all(full, 'modes', split_axis=0, concat_axis=2, tiled=True)[0]  17.7 us
    unnamed x98, local copies, waits for them, and re-layouts  16.5 us
    all_to_all x2, starting transfers between devices, body(): back = lax.all_to_all(out, 'modes', split_axis=1, concat_axis=1, tiled=True)  12.9 us
    ppermute x2, starting transfers between devices, body(): high = lax.ppermute(u_field[:1], flat, up)  12.4 us
    all_to_all x1, starting transfers between devices, body(): lax.all_to_all(jnp.broadcast_to(block_inverse, (devs,) + block_inverse.sh...  12.1 us
    ppermute x2, starting transfers between devices, body(): fill_l = lax.ppermute(u_field[..., -1], flat, rightward)  10.4 us
    slice x6, local copies, waits for them, and re-layouts, laplace_rows(): return 4.0 * center - padded[2:] - padded[:-2] - right - left  6.55 us
  transfers between devices with their start and end apart: 15, of which 6 were waited for; matrix products, arithmetic and copies ran while one was open for 34% of the time, Pallas kernels for 0%

profile of v3, /device:TPU:26, one launch (start us, length us, event | category | flops | bytes accessed | tf_op | source)
XLA Modules:
  0.0 211.2 jit_solution(15876779950090970999)
XLA Ops:
  0.0 1.1 fusion.94
  1.2 1.9 collective-permute-start
  3.1 3.6 %collective-permute-start.1 = (bf16[2,1,16,512]{3,1,2,0:T(2,128)(2,1)S(1)}, bf16[2,1,16,512]{3,1,2,0:T(2,128)(2,1)S(1)}, u32[]{:S(2)}, u32[]{:S(2)}) collective-permute-start(bf16[2,1,16,512]{3,1,2,0:T(2,128)(2,1)S(1)} %get-tuple-element.50), channel_id=1, source_target_pairs={{16,0},{32,16},{48,32},{64,48},{80,64},{96,80},{112,96},{128,112},... | collective-permute-start | bytes 98312 | tf_op jit(solution)/shard_map/ppermute | solution.py:15
  8.2 12.1 %all-to-all-start.1 = ((f32[16,1,256]{2,1,0:T(1,128)}), f32[16,1,256]{2,1,0:T(1,128)S(1)}, u32[]{:S(2)}, u32[]{:S(2)}) async-start(f32[16,1,256]{2,1,0:T(1,128)} %reshape.188), calls=%async_computation.1 | async-start | bytes 32768 | tf_op jit(solution)/shard_map/all_to_all | solution.py:55
  20.3 1.9 slice_bitcast_fusion.9
  34.7 9.7 %all-to-all-start = ((bf16[16,11,16,128]{3,2,1,0:T(8,128)(2,1)}), bf16[16,11,16,128]{3,2,1,0:T(8,128)(2,1)}, u32[]{:S(2)}, u32[]{:S(2)}) async-start(bf16[16,11,16,128]{3,2,1,0:T(8,128)(2,1)} %bitcast.10), calls=%async_computation | async-start | bytes 1441792 | tf_op jit(solution)/shard_map/all_to_all | solution.py:109
  47.1 3.0 %mul.516 = bf16[3,256,256]{2,1,0:T(8,128)(2,1)S(1)} reshape(bf16[3,16,16,16,16]{4,3,2,1,0:T(8,128)(2,1)S(1)} %mul.515) | data formatting | bytes 786432 | tf_op jit(solution)/shard_map/mul | solution.py:39
  50.2 1.1 concatenate.105
  52.2 1.2 copy.133
  54.2 1.2 copy.134
  55.3 1.7 reshape_squeeze.7
  59.6 1.9 slice.370
  61.5 1.9 slice.372
  67.3 1.5 all-to-all-done
  68.8 8.1 %all-to-all-start.3 = ((bf16[16,11,16,128]{3,2,1,0:T(8,128)(2,1)}), bf16[16,11,16,128]{3,2,1,0:T(8,128)(2,1)S(1)}, u32[]{:S(2)}, u32[]{:S(2)}) async-start(bf16[16,11,16,128]{3,2,1,0:T(8,128)(2,1)} %bitcast.64), calls=%async_computation.3 | async-start | bytes 1441792 | tf_op jit(solution)/shard_map/all_to_all | solution.py:109
  76.9 1.3 copy.188
  78.3 1.2 fusion.82
  79.6 1.2 copy.109
  80.9 2.0 copy.110
  82.9 1.2 fusion.83
  84.1 1.3 copy.161
  85.4 2.1 copy.164
  90.3 2.0 fusion.52
  93.4 1.8 fusion.27
  95.2 1.3 fusion.98
  97.9 1.0 fusion.87
  98.9 1.9 all-to-all-done.3
  103.3 1.2 copy.148
  105.8 1.0 fusion.86
  106.8 2.1 %copy.167 = f32[4,256,127]{1,2,0:T(8,128)} copy(f32[4,256,127]{2,1,0:T(8,128)} %get-tuple-element.30) | data formatting | bytes 1040384
  108.9 1.0 copy.170
  112.4 1.3 fusion.53
  116.5 1.3 collective-permute-start.4
  117.8 2.8 %collective-permute-start.3 = (f32[1,256,128]{1,2,0:T(8,128)S(1)}, f32[1,256,128]{1,2,0:T(8,128)S(1)}, u32[]{:S(2)}, u32[]{:S(2)}) collective-permute-start(f32[1,256,128]{1,2,0:T(8,128)S(1)} %copy-done.18), channel_id=1, source_target_pairs={{0,4},{1,5},{2,6},{3,7},{4,8},{5,9},{6,10},{7,11},{8,12},{9,13},{1... | collective-permute-start | bytes 393224 | tf_op jit(solution)/shard_map/ppermute | solution.py:122
  120.7 5.7 %collective-permute-start.2 = (f32[1,256,128]{1,2,0:T(8,128)S(1)}, f32[1,256,128]{1,2,0:T(8,128)S(1)}, u32[]{:S(2)}, u32[]{:S(2)}) collective-permute-start(f32[1,256,128]{1,2,0:T(8,128)S(1)} %copy-done.17), channel_id=1, source_target_pairs={{4,0},{5,1},{6,2},{7,3},{8,4},{9,5},{10,6},{11,7},{12,8},{13,9},{1... | collective-permute-start | bytes 393224 | tf_op jit(solution)/shard_map/ppermute | solution.py:123
  126.5 6.1 %collective-permute-start.5 = (f32[4,256]{1,0:T(4,128)S(1)}, f32[4,256]{1,0:T(4,128)S(1)}, u32[]{:S(2)}, u32[]{:S(2)}) collective-permute-start(f32[4,256]{1,0:T(4,128)S(1)} %bitcast.300), channel_id=1, source_target_pairs={{0,1},{1,2},{2,3},{4,5},{5,6},{6,7},{8,9},{9,10},{10,11},{12,13},{... | collective-permute-start | bytes 12296 | tf_op jit(solution)/shard_map/ppermute | solution.py:124
  132.5 1.9 collective-permute-start.7
  134.5 6.7 %collective-permute-start.6 = (f32[1,256,128]{1,2,0:T(8,128)}, f32[1,256,128]{1,2,0:T(8,128)}, u32[]{:S(2)}, u32[]{:S(2)}) collective-permute-start(f32[1,256,128]{1,2,0:T(8,128)} %get-tuple-element.48), channel_id=1, source_target_pairs={{4,0},{5,1},{6,2},{7,3},{8,4},{9,5},{10,6},{11,7},{12,8},{13,9},{1... | collective-permute-start | bytes 393224 | tf_op jit(solution)/shard_map/ppermute | solution.py:123
  141.2 4.3 %collective-permute-start.9 = (f32[4,256]{1,0:T(4,128)S(1)}, f32[4,256]{1,0:T(4,128)S(1)}, u32[]{:S(2)}, u32[]{:S(2)}) collective-permute-start(f32[4,256]{1,0:T(4,128)S(1)} %bitcast.301), channel_id=1, source_target_pairs={{0,1},{1,2},{2,3},{4,5},{5,6},{6,7},{8,9},{9,10},{10,11},{12,13},{... | collective-permute-start | bytes 12296 | tf_op jit(solution)/shard_map/ppermute | solution.py:124
  145.5 1.3 collective-permute-done.9
  146.8 1.3 collective-permute-start.8
  148.8 5.3 %collective-permute-done.8 = f32[4,256]{1,0:T(4,128)S(1)} collective-permute-done((f32[4,256]{1,0:T(4,128)S(1)}, f32[4,256]{1,0:T(4,128)S(1)}, u32[]{:S(2)}, u32[]{:S(2)}) %collective-permute-start.8) | collective-permute-done | bytes 4128 | tf_op jit(solution)/shard_map/ppermute | solution.py:125
  159.7 9.4 %all-to-all-start.2 = ((f32[4,16,16,128]{3,2,0,1:T(8,128)}), f32[4,16,16,128]{3,2,0,1:T(8,128)S(1)}, u32[]{:S(2)}, u32[]{:S(2)}) async-start(f32[4,16,16,128]{3,2,0,1:T(8,128)} %copy.131), calls=%async_computation.2 | async-start | bytes 1048576 | tf_op jit(solution)/shard_map/all_to_all | solution.py:147
  172.6 1.5 fusion.15
  175.8 11.9 %all-to-all-done.2 = f32[4,16,16,128]{3,2,0,1:T(8,128)S(1)} async-done(((f32[4,16,16,128]{3,2,0,1:T(8,128)}), f32[4,16,16,128]{3,2,0,1:T(8,128)S(1)}, u32[]{:S(2)}, u32[]{:S(2)}) %all-to-all-start.2) | async-done | bytes 524320 | tf_op jit(solution)/shard_map/all_to_all | solution.py:147
  187.7 3.6 %all-to-all-start.4 = ((f32[4,16,16,128]{3,2,0,1:T(8,128)}), f32[4,16,16,128]{3,2,0,1:T(8,128)S(1)}, u32[]{:S(2)}, u32[]{:S(2)}) async-start(f32[4,16,16,128]{3,2,0,1:T(8,128)} %copy.155), calls=%async_computation.4 | async-start | bytes 1048576 | tf_op jit(solution)/shard_map/all_to_all | solution.py:147
  191.9 17.7 %all-to-all-done.4 = f32[4,16,16,128]{3,2,0,1:T(8,128)S(1)} async-done(((f32[4,16,16,128]{3,2,0,1:T(8,128)}), f32[4,16,16,128]{3,2,0,1:T(8,128)S(1)}, u32[]{:S(2)}, u32[]{:S(2)}) %all-to-all-start.4) | async-done | bytes 524320 | tf_op jit(solution)/shard_map/all_to_all | solution.py:147
  210.2 1.0 pad_maximum_fusion
  (221 shorter events, 51.4 us)
Async XLA Ops:
  0.0 22.2 %copy-start.23 = (s32[16,512]{1,0:T(8,128)S(1)}, s32[16,512]{1,0:T(8,128)}, u32[]{:S(2)}) copy-start(s32[16,512]{1,0:T(8,128)} %param.10) | copy-start | bytes 98308
  0.0 22.6 %copy-start.16 = (f32[2,3,8]{2,0,1:T(2,128)S(1)}, f32[2,3,8]{2,0,1:T(2,128)}, u32[]{:S(2)}) copy-start(f32[2,3,8]{2,0,1:T(2,128)} %param.12) | copy-start | bytes 580
  1.1 23.2 %copy-start.19 = (f32[2,8]{1,0:T(2,128)S(1)}, f32[2,8]{1,0:T(2,128)}, u32[]{:S(2)}) copy-start(f32[2,8]{1,0:T(2,128)} %param.11) | copy-start | bytes 196
  1.2 27.5 %collective-permute-start = (bf16[2,1,16,512]{3,1,2,0:T(2,128)(2,1)S(1)}, bf16[2,1,16,512]{3,1,2,0:T(2,128)(2,1)S(1)}, u32[]{:S(2)}, u32[]{:S(2)}) collective-permute-start(bf16[2,1,16,512]{3,1,2,0:T(2,128)(2,1)S(1)} %get-tuple-element.49), channel_id=1, source_target_pairs={{0,16},{16,32},{32,48},{48,64},{64,80},{80,96},{96,112},{112,128},... | collective-permute-start | bytes 98312 | tf_op jit(solution)/shard_map/ppermute | solution.py:14
  3.1 25.6 %collective-permute-start.1 = (bf16[2,1,16,512]{3,1,2,0:T(2,128)(2,1)S(1)}, bf16[2,1,16,512]{3,1,2,0:T(2,128)(2,1)S(1)}, u32[]{:S(2)}, u32[]{:S(2)}) collective-permute-start(bf16[2,1,16,512]{3,1,2,0:T(2,128)(2,1)S(1)} %get-tuple-element.50), channel_id=1, source_target_pairs={{16,0},{32,16},{48,32},{64,48},{80,64},{96,80},{112,96},{128,112},... | collective-permute-start | bytes 98312 | tf_op jit(solution)/shard_map/ppermute | solution.py:15
  8.2 17.3 %copy-start.9 = (bf16[2,16,16,512]{3,2,1,0:T(8,128)(2,1)S(1)}, bf16[2,16,16,512]{3,2,1,0:T(8,128)(2,1)}, u32[]{:S(2)}) copy-start(bf16[2,16,16,512]{3,2,1,0:T(8,128)(2,1)} %param.8) | copy-start | bytes 1572868
  8.2 26.5 %all-to-all-start.1 = ((f32[16,1,256]{2,1,0:T(1,128)}), f32[16,1,256]{2,1,0:T(1,128)S(1)}, u32[]{:S(2)}, u32[]{:S(2)}) async-start(f32[16,1,256]{2,1,0:T(1,128)} %reshape.188), calls=%async_computation.1 | async-start | bytes 32768 | tf_op jit(solution)/shard_map/all_to_all | solution.py:55
  24.6 4.1 %copy-start.1 = (bf16[2,16,16,512]{3,2,1,0:T(8,128)(2,1)S(1)}, bf16[2,16,16,512]{3,2,1,0:T(8,128)(2,1)}, u32[]{:S(2)}) copy-start(bf16[2,16,16,512]{3,2,1,0:T(8,128)(2,1)} %param.9) | copy-start | bytes 1572868
  31.5 15.1 %copy-start.24 = (s32[3,16,16]{2,1,0:T(8,128)S(1)}, s32[3,16,16]{2,1,0:T(8,128)}, u32[]{:S(2)}) copy-start(s32[3,16,16]{2,1,0:T(8,128)} %param.14) | copy-start | bytes 9220
  34.7 34.1 %all-to-all-start = ((bf16[16,11,16,128]{3,2,1,0:T(8,128)(2,1)}), bf16[16,11,16,128]{3,2,1,0:T(8,128)(2,1)}, u32[]{:S(2)}, u32[]{:S(2)}) async-start(bf16[16,11,16,128]{3,2,1,0:T(8,128)(2,1)} %bitcast.10), calls=%async_computation | async-start | bytes 1441792 | tf_op jit(solution)/shard_map/all_to_all | solution.py:109
  50.1 6.9 %copy-start.13 = (bf16[3,256,256]{2,1,0:T(8,128)(2,1)S(1)}, bf16[3,256,256]{2,1,0:T(8,128)(2,1)}, u32[]{:S(2)}) copy-start(bf16[3,256,256]{2,1,0:T(8,128)(2,1)} %param.13) | copy-start | bytes 1179652
  50.2 8.3 %copy-start.20 = (f32[16,16]{1,0:T(8,128)S(1)}, f32[16,16]{1,0:T(8,128)}, u32[]{:S(2)}) copy-start(f32[16,16]{1,0:T(8,128)} %fusion.74) | copy-start | bytes 3076
  58.7 7.0 %copy-start.14 = (bf16[4,4,16,4]{1,2,3,0:T(8,128)(2,1)S(1)}, bf16[4,4,16,4]{1,2,3,0:T(8,128)(2,1)}, u32[]{:S(2)}) copy-start(bf16[4,4,16,4]{1,2,3,0:T(8,128)(2,1)} %copy.133) | copy-start | bytes 6148
  58.7 7.0 %copy-start.15 = (bf16[4,4,16,4]{1,2,3,0:T(8,128)(2,1)S(1)}, bf16[4,4,16,4]{1,2,3,0:T(8,128)(2,1)}, u32[]{:S(2)}) copy-start(bf16[4,4,16,4]{1,2,3,0:T(8,128)(2,1)} %copy.134) | copy-start | bytes 6148
  58.7 7.7 %copy-start.7 = (bf16[16,4,4,4,128]{4,3,2,1,0:T(4,128)(2,1)S(1)}, bf16[16,4,4,4,128]{4,3,2,1,0:T(4,128)(2,1)}, u32[]{:S(2)}) copy-start(bf16[16,4,4,4,128]{4,3,2,1,0:T(4,128)(2,1)} %reshape_squeeze.7) | copy-start | bytes 786436
  68.8 32.0 %all-to-all-start.3 = ((bf16[16,11,16,128]{3,2,1,0:T(8,128)(2,1)}), bf16[16,11,16,128]{3,2,1,0:T(8,128)(2,1)S(1)}, u32[]{:S(2)}, u32[]{:S(2)}) async-start(bf16[16,11,16,128]{3,2,1,0:T(8,128)(2,1)} %bitcast.64), calls=%async_computation.3 | async-start | bytes 1441792 | tf_op jit(solution)/shard_map/all_to_all | solution.py:109
  78.2 1.3 copy-start
  84.1 6.2 %copy-start.5 = (f32[4,256,128]{1,2,0:T(8,128)S(1)}, f32[4,256,128]{1,2,0:T(8,128)}, u32[]{:S(2)}) copy-start(f32[4,256,128]{1,2,0:T(8,128)} %copy.110) | copy-start | bytes 1572868
  90.2 3.2 %copy-start.22 = (f32[4,3,128]{2,1,0:T(4,128)S(1)}, f32[4,3,128]{2,1,0:T(4,128)}, u32[]{:S(2)}) copy-start(f32[4,3,128]{2,1,0:T(4,128)} %get-tuple-element.63) | copy-start | bytes 18436
  90.2 3.2 %copy-start.33 = (f32[4,128]{1,0:T(4,128)S(1)}, f32[4,128]{1,0:T(4,128)}, u32[]{:S(2)}) copy-start(f32[4,128]{1,0:T(4,128)} %get-tuple-element.65) | copy-start | bytes 6148
  90.2 3.2 %copy-start.35 = (f32[4,128]{1,0:T(4,128)S(1)}, f32[4,128]{1,0:T(4,128)}, u32[]{:S(2)}) copy-start(f32[4,128]{1,0:T(4,128)} %get-tuple-element.67) | copy-start | bytes 6148
  93.4 3.2 %copy-start.2 = (f32[4,256,128]{1,2,0:T(8,128)}, f32[4,256,128]{1,2,0:T(8,128)S(1)}, u32[]{:S(2)}) copy-start(f32[4,256,128]{1,2,0:T(8,128)S(1)} %copy.115) | copy-start | bytes 1572868
  106.8 5.5 %copy-start.6 = (bf16[1,4,16,16,128]{4,3,2,1,0:T(8,128)(2,1)S(1)}, bf16[1,4,16,16,128]{4,3,2,1,0:T(8,128)(2,1)}, u32[]{:S(2)}) copy-start(bf16[1,4,16,16,128]{4,3,2,1,0:T(8,128)(2,1)} %slice.438) | copy-start | bytes 786436
  108.9 3.5 %copy-start.4 = (f32[4,256,128]{1,2,0:T(8,128)S(1)}, f32[4,256,128]{1,2,0:T(8,128)}, u32[]{:S(2)}) copy-start(f32[4,256,128]{1,2,0:T(8,128)} %copy.141) | copy-start | bytes 1572868
  112.4 1.4 copy-start.21
  112.4 1.4 copy-start.29
  112.4 1.4 copy-start.31
  114.9 1.7 copy-start.28
  114.9 3.0 %copy-start.18 = (f32[1,256,128]{1,2,0:T(8,128)S(1)}, f32[1,256,128]{1,2,0:T(8,128)}, u32[]{:S(2)}) copy-start(f32[1,256,128]{1,2,0:T(8,128)} %get-tuple-element.35) | copy-start | bytes 393220
  114.9 5.8 %copy-start.17 = (f32[1,256,128]{1,2,0:T(8,128)S(1)}, f32[1,256,128]{1,2,0:T(8,128)}, u32[]{:S(2)}) copy-start(f32[1,256,128]{1,2,0:T(8,128)} %get-tuple-element.36) | copy-start | bytes 393220
  114.9 11.6 %copy-start.27 = (f32[4,256,1]{1,2,0:T(1,128)S(1)}, f32[4,256,1]{1,2,0:T(1,128)}, u32[]{:S(2)}) copy-start(f32[4,256,1]{1,2,0:T(1,128)} %get-tuple-element.33) | copy-start | bytes 12292
  114.9 41.0 %copy-start.8 = (bf16[4,256,128]{1,2,0:T(8,128)(2,1)S(1)}, bf16[4,256,128]{1,2,0:T(8,128)(2,1)}, u32[]{:S(2)}) copy-start(bf16[4,256,128]{1,2,0:T(8,128)(2,1)} %get-tuple-element.77) | copy-start | bytes 786436
  116.5 17.9 %collective-permute-start.4 = (f32[4,256]{1,0:T(4,128)S(1)}, f32[4,256]{1,0:T(4,128)S(1)}, u32[]{:S(2)}, u32[]{:S(2)}) collective-permute-start(f32[4,256]{1,0:T(4,128)S(1)} %bitcast.299), channel_id=1, source_target_pairs={{1,0},{2,1},{3,2},{5,4},{6,5},{7,6},{9,8},{10,9},{11,10},{13,12},{... | collective-permute-start | bytes 12296 | tf_op jit(solution)/shard_map/ppermute | solution.py:125
  117.8 38.0 %collective-permute-start.3 = (f32[1,256,128]{1,2,0:T(8,128)S(1)}, f32[1,256,128]{1,2,0:T(8,128)S(1)}, u32[]{:S(2)}, u32[]{:S(2)}) collective-permute-start(f32[1,256,128]{1,2,0:T(8,128)S(1)} %copy-done.18), channel_id=1, source_target_pairs={{0,4},{1,5},{2,6},{3,7},{4,8},{5,9},{6,10},{7,11},{8,12},{9,13},{1... | collective-permute-start | bytes 393224 | tf_op jit(solution)/shard_map/ppermute | solution.py:122
  120.7 35.2 %collective-permute-start.2 = (f32[1,256,128]{1,2,0:T(8,128)S(1)}, f32[1,256,128]{1,2,0:T(8,128)S(1)}, u32[]{:S(2)}, u32[]{:S(2)}) collective-permute-start(f32[1,256,128]{1,2,0:T(8,128)S(1)} %copy-done.17), channel_id=1, source_target_pairs={{4,0},{5,1},{6,2},{7,3},{8,4},{9,5},{10,6},{11,7},{12,8},{13,9},{1... | collective-permute-start | bytes 393224 | tf_op jit(solution)/shard_map/ppermute | solution.py:123
  126.5 14.7 %collective-permute-start.5 = (f32[4,256]{1,0:T(4,128)S(1)}, f32[4,256]{1,0:T(4,128)S(1)}, u32[]{:S(2)}, u32[]{:S(2)}) collective-permute-start(f32[4,256]{1,0:T(4,128)S(1)} %bitcast.300), channel_id=1, source_target_pairs={{0,1},{1,2},{2,3},{4,5},{5,6},{6,7},{8,9},{9,10},{10,11},{12,13},{... | collective-permute-start | bytes 12296 | tf_op jit(solution)/shard_map/ppermute | solution.py:124
  132.5 36.5 %collective-permute-start.7 = (f32[1,256,128]{1,2,0:T(8,128)}, f32[1,256,128]{1,2,0:T(8,128)}, u32[]{:S(2)}, u32[]{:S(2)}) collective-permute-start(f32[1,256,128]{1,2,0:T(8,128)} %get-tuple-element.47), channel_id=1, source_target_pairs={{0,4},{1,5},{2,6},{3,7},{4,8},{5,9},{6,10},{7,11},{8,12},{9,13},{1... | collective-permute-start | bytes 393224 | tf_op jit(solution)/shard_map/ppermute | solution.py:122
  134.5 35.5 %collective-permute-start.6 = (f32[1,256,128]{1,2,0:T(8,128)}, f32[1,256,128]{1,2,0:T(8,128)}, u32[]{:S(2)}, u32[]{:S(2)}) collective-permute-start(f32[1,256,128]{1,2,0:T(8,128)} %get-tuple-element.48), channel_id=1, source_target_pairs={{4,0},{5,1},{6,2},{7,3},{8,4},{9,5},{10,6},{11,7},{12,8},{13,9},{1... | collective-permute-start | bytes 393224 | tf_op jit(solution)/shard_map/ppermute | solution.py:123
  141.2 5.7 %collective-permute-start.9 = (f32[4,256]{1,0:T(4,128)S(1)}, f32[4,256]{1,0:T(4,128)S(1)}, u32[]{:S(2)}, u32[]{:S(2)}) collective-permute-start(f32[4,256]{1,0:T(4,128)S(1)} %bitcast.301), channel_id=1, source_target_pairs={{0,1},{1,2},{2,3},{4,5},{5,6},{6,7},{8,9},{9,10},{10,11},{12,13},{... | collective-permute-start | bytes 12296 | tf_op jit(solution)/shard_map/ppermute | solution.py:124
  146.8 7.3 %collective-permute-start.8 = (f32[4,256]{1,0:T(4,128)S(1)}, f32[4,256]{1,0:T(4,128)S(1)}, u32[]{:S(2)}, u32[]{:S(2)}) collective-permute-start(f32[4,256]{1,0:T(4,128)S(1)} %bitcast.298), channel_id=1, source_target_pairs={{1,0},{2,1},{3,2},{5,4},{6,5},{7,6},{9,8},{10,9},{11,10},{13,12},{... | collective-permute-start | bytes 12296 | tf_op jit(solution)/shard_map/ppermute | solution.py:125
  156.1 1.0 copy-start.3
  156.1 1.2 copy-start.10
  156.1 1.3 copy-start.11
  156.1 1.3 copy-start.34
  156.1 1.3 copy-start.36
  159.7 28.1 %all-to-all-start.2 = ((f32[4,16,16,128]{3,2,0,1:T(8,128)}), f32[4,16,16,128]{3,2,0,1:T(8,128)S(1)}, u32[]{:S(2)}, u32[]{:S(2)}) async-start(f32[4,16,16,128]{3,2,0,1:T(8,128)} %copy.131), calls=%async_computation.2 | async-start | bytes 1048576 | tf_op jit(solution)/shard_map/all_to_all | solution.py:147
  171.6 1.0 copy-start.32
  187.7 21.9 %all-to-all-start.4 = ((f32[4,16,16,128]{3,2,0,1:T(8,128)}), f32[4,16,16,128]{3,2,0,1:T(8,128)S(1)}, u32[]{:S(2)}, u32[]{:S(2)}) async-start(f32[4,16,16,128]{3,2,0,1:T(8,128)} %copy.155), calls=%async_computation.4 | async-start | bytes 1048576 | tf_op jit(solution)/shard_map/all_to_all | solution.py:147
  (6 other events, 5.5 us)

commit v4 on v2

--- a/solution.py
+++ b/solution.py
@@ -52,7 +52,10 @@
     my_r = me // col_chunks
     my_c = me % col_chunks
 
-    every = lax.all_gather(block_inverse, "modes", tiled=True)
+    every = lax.all_to_all(
+        jnp.broadcast_to(block_inverse, (devs,) + block_inverse.shape[1:]),
+        "modes", split_axis=0, concat_axis=0, tiled=True,
+    )
     eye = jnp.eye(blocks, dtype=jnp.float32)
     dense_inv = (every[:, :, None, :] * eye[:, None, :, None]).reshape(modes_all, modes_all)
 
@@ -67,31 +70,7 @@
     coef = coef.transpose(0, 2, 1, 3)[:, :, :, None, :]
     inverse_base = 1.0 / (4.0 * base)
 
-    rhs_p = rhs.reshape(fields, modes_dev, row_chunks, rows_c, col_chunks, LANES)
-    rhs_p = rhs_p.transpose(0, 3, 2, 4, 1, 5).reshape(fields, rows_c, devs, modes_dev, LANES)
-    rhs_c = lax.all_to_all(rhs_p, "modes", split_axis=2, concat_axis=3, tiled=True)[:, :, 0]
-    rhs_c = rhs_c.astype(jnp.float32)
-
     init_x = ring_halo(initial.transpose(0, 2, 1, 3), "space", 1)
-    zero_col = jnp.zeros((fields, rows_c, modes_dev), init_x.dtype)
-    pieces = []
-    for r in range(row_chunks):
-        for c in range(col_chunks):
-            main = init_x[:, r * rows_c : r * rows_c + rows_c + 2, :, c * LANES : (c + 1) * LANES]
-            inner = init_x[:, r * rows_c + 1 : r * rows_c + rows_c + 1]
-            hl = inner[..., c * LANES - 1] if c > 0 else zero_col
-            hr = inner[..., (c + 1) * LANES] if c < col_chunks - 1 else zero_col
-            side = jnp.concatenate([hl, hr], axis=1).transpose(0, 2, 1)
-            side = jnp.pad(side, ((0, 0), (0, 0), (0, LANES - 2 * rows_c)))[:, None]
-            pieces.append(jnp.concatenate([main, side], axis=1))
-    stacked = jnp.stack(pieces, axis=2)
-    got = lax.all_to_all(stacked, "modes", split_axis=2, concat_axis=3, tiled=True)[:, :, 0]
-    got = got.astype(jnp.float32)
-    side = got[:, rows_c + 2]
-    fill_l = side[..., :rows_c].transpose(0, 2, 1)
-    fill_r = side[..., rows_c : 2 * rows_c].transpose(0, 2, 1)
-    padded = got[:, : rows_c + 2]
-    u_field = padded[:, 1:-1]
 
     flat = ("space", "modes")
     total_rc = spaces * row_chunks
@@ -110,6 +89,34 @@
     ]
     leftward = [(b, a) for a, b in rightward]
 
+    def pack(init_f, rhs_f):
+        top = init_f[:, 0 : rows : rows_c]
+        mid = init_f[:, 1 : rows + 1].reshape(fields, row_chunks, rows_c, modes_dev, cols)
+        bot = init_f[:, rows_c + 1 : rows + 2 : rows_c]
+        main = jnp.concatenate([top[:, :, None], mid, bot[:, :, None]], axis=2)
+        main = main.reshape(fields, row_chunks, rows_c + 2, modes_dev, col_chunks, LANES)
+        inner = init_f[:, 1 : rows + 1]
+        hl = jnp.pad(inner[..., LANES - 1 : cols - 1 : LANES], ((0, 0), (0, 0), (0, 0), (1, 0)))
+        hr = jnp.pad(inner[..., LANES : cols : LANES], ((0, 0), (0, 0), (0, 0), (0, 1)))
+        sides = []
+        for h in (hl, hr):
+            h = h.reshape(fields, row_chunks, rows_c, modes_dev, col_chunks)
+            sides.append(h.transpose(0, 1, 3, 4, 2))
+        side = jnp.concatenate(sides, axis=-1)
+        side = jnp.pad(side, ((0, 0),) * 4 + ((0, LANES - 2 * rows_c),))[:, :, None]
+        rp = rhs_f.reshape(fields, modes_dev, row_chunks, rows_c, col_chunks, LANES)
+        rp = rp.transpose(0, 2, 3, 1, 4, 5)
+        full = jnp.concatenate([main, side, rp], axis=2)
+        full = full.transpose(1, 4, 0, 2, 3, 5).reshape(devs, fields, -1, modes_dev, LANES)
+        return lax.all_to_all(full, "modes", split_axis=0, concat_axis=3, tiled=True)[0]
+
+    got = pack(init_x, rhs)
+    padded = got[:, : rows_c + 2].astype(jnp.float32)
+    side = got[:, rows_c + 2].astype(jnp.float32)
+    fill_l = side[..., :rows_c].transpose(0, 2, 1)
+    fill_r = side[..., rows_c : 2 * rows_c].transpose(0, 2, 1)
+    rhs_c = got[:, rows_c + 3 :].astype(jnp.float32)
+    u_field = padded[:, 1:-1]
     for sweep in range(SWEEPS):
         if sweep > 0:
             low = lax.ppermute(u_field[:, -1:], flat, down)

time: 191 us -> 161 us (0.84)
  the two profiles are of different devices: /device:TPU:56 before, /device:TPU:25 now
where the time goes in v4:
time: 161 us; the launch traced here: 160 us
  starting transfers between devices  44.6 us (28%)
  blocking collectives  41.5 us (26%)
  local copies, waits for them, and re-layouts  32.4 us (20%)
  waiting for transfers between devices  31.6 us (20%)
  other arithmetic  5.31 us (3%)
  matrix products  4.08 us (3%)
    all_to_all x1, blocking collectives, body(): back = lax.all_to_all(out, 'modes', split_axis=2, concat_axis=2, tiled=True)  41.5 us
    all_to_all x1, waiting for transfers between devices, pack(): lax.all_to_all(full, 'modes', split_axis=0, concat_axis=3, tiled=True)[0]  24.4 us
    all_to_all x1, starting transfers between devices, body(): lax.all_to_all(jnp.broadcast_to(block_inverse, (devs,) + block_inverse.sh...  12.3 us
    all_to_all x1, starting transfers between devices, pack(): lax.all_to_all(full, 'modes', split_axis=0, concat_axis=3, tiled=True)[0]  9.24 us
    ppermute x1, waiting for transfers between devices, body(): low = lax.ppermute(u_field[:, -1:], flat, down)  7.25 us
    ppermute x1, starting transfers between devices, body(): high = lax.ppermute(u_field[:, :1], flat, up)  6.2 us
    ppermute x1, starting transfers between devices, body(): fill_l = lax.ppermute(u_field[..., -1], flat, rightward)  5.49 us
    unnamed x32, local copies, waits for them, and re-layouts  5.19 us
  transfers between devices with their start and end apart: 8, of which 2 were waited for; matrix products, arithmetic and copies ran while one was open for 16% of the time, Pallas kernels for 0%

profile of v4, /device:TPU:25, one launch (start us, length us, event | category | flops | bytes accessed | tf_op | source)
XLA Modules:
  0.0 160.3 jit_solution(2971350851489620995)
XLA Ops:
  0.0 1.2 fusion.60
  1.2 3.7 %collective-permute-start = (bf16[2,1,16,512]{3,1,2,0:T(2,128)(2,1)S(1)}, bf16[2,1,16,512]{3,1,2,0:T(2,128)(2,1)S(1)}, u32[]{:S(2)}, u32[]{:S(2)}) collective-permute-start(bf16[2,1,16,512]{3,1,2,0:T(2,128)(2,1)S(1)} %get-tuple-element.25), channel_id=1, source_target_pairs={{0,16},{16,32},{32,48},{48,64},{64,80},{80,96},{96,112},{112,128},... | collective-permute-start | bytes 98312 | tf_op jit(solution)/shard_map/ppermute | solution.py:14
  4.9 1.9 %collective-permute-start.1 = (bf16[2,1,16,512]{3,1,2,0:T(2,128)(2,1)S(1)}, bf16[2,1,16,512]{3,1,2,0:T(2,128)(2,1)S(1)}, u32[]{:S(2)}, u32[]{:S(2)}) collective-permute-start(bf16[2,1,16,512]{3,1,2,0:T(2,128)(2,1)S(1)} %get-tuple-element.26), channel_id=1, source_target_pairs={{16,0},{32,16},{48,32},{64,48},{80,64},{96,80},{112,96},{128,112},... | collective-permute-start | bytes 98312 | tf_op jit(solution)/shard_map/ppermute | solution.py:15
  6.8 0.7 broadcast_in_dim.28
  7.5 0.7 reshape.115
  8.2 12.3 %all-to-all-start.1 = ((f32[16,1,256]{2,1,0:T(1,128)}), f32[16,1,256]{2,1,0:T(1,128)S(1)}, u32[]{:S(2)}, u32[]{:S(2)}) async-start(f32[16,1,256]{2,1,0:T(1,128)} %reshape.115), calls=%async_computation.1 | async-start | bytes 32768 | tf_op jit(solution)/shard_map/all_to_all | solution.py:55
  20.6 2.2 %slice.146 = bf16[2,16,16,3]{3,1,2,0:T(8,128)(2,1)S(1)} slice(bf16[2,16,16,512]{3,1,2,0:T(8,128)(2,1)} %bitcast.135), slice={[0:2:1], [0:16:1], [0:16:1], [127:511:128]} | slice | bytes 6144 | tf_op jit(solution)/shard_map/slice | solution.py:99
  22.8 2.1 %slice.147 = bf16[2,16,16,3]{3,1,2,0:T(8,128)(2,1)S(1)} slice(bf16[2,16,16,512]{3,1,2,0:T(8,128)(2,1)} %bitcast.136), slice={[0:2:1], [0:16:1], [0:16:1], [128:512:128]} | slice | bytes 6144 | tf_op jit(solution)/shard_map/slice | solution.py:100
  24.9 1.2 concatenate.48
  26.3 1.0 copy.60
  27.3 1.0 copy.61
  28.5 0.4 pad_maximum_fusion.2
  29.0 0.8 slice.145
  29.7 0.8 slice.144
  30.6 0.7 copy_dynamic-update-slice_fusion.2
  31.3 1.2 copy_dynamic-update-slice_fusion
  32.5 0.7 copy_dynamic-update-slice_fusion.1
  33.2 0.8 fusion.41
  34.0 1.2 bitcast_dynamic-update-slice_fusion
  35.3 9.2 %all-to-all-start = ((bf16[16,2,11,16,128]{4,3,2,1,0:T(8,128)(2,1)}), bf16[16,2,11,16,128]{4,3,2,1,0:T(8,128)(2,1)}, u32[]{:S(2)}, u32[]{:S(2)}) async-start(bf16[16,2,11,16,128]{4,3,2,1,0:T(8,128)(2,1)} %bitcast.8), calls=%async_computation | async-start | bytes 2883584 | tf_op jit(solution)/shard_map/all_to_all | solution.py:111
  45.9 0.5 mul.428
  46.4 3.7 %mul.429 = bf16[3,256,256]{2,1,0:T(8,128)(2,1)} reshape(bf16[3,16,16,16,16]{4,3,2,1,0:T(8,128)(2,1)S(1)} %mul.428) | data formatting | bytes 786432 | tf_op jit(solution)/shard_map/mul | solution.py:39
  50.1 0.3 slice_reduce_fusion.4
  50.5 0.7 multiply_divide_fusion
  51.4 0.5 broadcast.106
  51.9 0.7 reduce.16
  52.9 1.5 reshape.104
  54.5 24.4 %all-to-all-done = bf16[16,2,11,16,128]{4,3,2,1,0:T(8,128)(2,1)} async-done(((bf16[16,2,11,16,128]{4,3,2,1,0:T(8,128)(2,1)}), bf16[16,2,11,16,128]{4,3,2,1,0:T(8,128)(2,1)}, u32[]{:S(2)}, u32[]{:S(2)}) %all-to-all-start) | async-done | bytes 1441824 | tf_op jit(solution)/shard_map/all_to_all | solution.py:111
  78.8 1.7 %copy.66 = bf16[16,2,11,16,128]{4,3,0,2,1:T(8,128)(2,1)S(1)} copy(bf16[16,2,11,16,128]{4,3,2,1,0:T(8,128)(2,1)} %all-to-all-done) | data formatting | bytes 2883584 | tf_op jit(solution)/shard_map/all_to_all | solution.py:111
  80.6 0.8 slice.191
  81.5 0.3 copy.90
  82.0 1.2 fusion.59
  83.3 1.2 copy.91
  84.6 1.6 fusion.30
  86.2 0.9 fusion.16
  87.2 1.0 fusion.62
  88.4 1.3 collective-permute-start.4
  89.8 5.5 %collective-permute-start.5 = (f32[2,4,256]{2,1,0:T(4,128)S(1)}, f32[2,4,256]{2,1,0:T(4,128)S(1)}, u32[]{:S(2)}, u32[]{:S(2)}) collective-permute-start(f32[2,4,256]{2,1,0:T(4,128)S(1)} %bitcast.147), channel_id=1, source_target_pairs={{0,1},{1,2},{2,3},{4,5},{5,6},{6,7},{8,9},{9,10},{10,11},{12,13},{... | collective-permute-start | bytes 24584 | tf_op jit(solution)/shard_map/ppermute | solution.py:124
  95.3 4.5 %collective-permute-start.3 = (f32[2,1,256,128]{2,3,1,0:T(8,128)S(1)}, f32[2,1,256,128]{2,3,1,0:T(8,128)S(1)}, u32[]{:S(2)}, u32[]{:S(2)}) collective-permute-start(f32[2,1,256,128]{2,3,1,0:T(8,128)S(1)} %get-tuple-element.21), channel_id=1, source_target_pairs={{0,4},{1,5},{2,6},{3,7},{4,8},{5,9},{6,10},{7,11},{8,12},{9,13},{1... | collective-permute-start | bytes 786440 | tf_op jit(solution)/shard_map/ppermute | solution.py:122
  99.8 6.2 %collective-permute-start.2 = (f32[2,1,256,128]{2,3,1,0:T(8,128)S(1)}, f32[2,1,256,128]{2,3,1,0:T(8,128)S(1)}, u32[]{:S(2)}, u32[]{:S(2)}) collective-permute-start(f32[2,1,256,128]{2,3,1,0:T(8,128)S(1)} %get-tuple-element.22), channel_id=1, source_target_pairs={{4,0},{5,1},{6,2},{7,3},{8,4},{9,5},{10,6},{11,7},{12,8},{13,9},{1... | collective-permute-start | bytes 786440 | tf_op jit(solution)/shard_map/ppermute | solution.py:123
  106.1 7.2 %collective-permute-done.3 = f32[2,1,256,128]{2,3,1,0:T(8,128)S(1)} collective-permute-done((f32[2,1,256,128]{2,3,1,0:T(8,128)S(1)}, f32[2,1,256,128]{2,3,1,0:T(8,128)S(1)}, u32[]{:S(2)}, u32[]{:S(2)}) %collective-permute-start.3) | collective-permute-done | bytes 262176 | tf_op jit(solution)/shard_map/ppermute | solution.py:122
  113.7 0.3 fusion.23
  114.0 1.1 fusion.21
  115.2 1.0 fusion.9
  116.2 0.3 copy.83
  116.7 41.5 %all_to_all.25 = f32[2,4,16,16,128]{4,3,1,0,2:T(8,128)S(1)} all-to-all(f32[2,4,16,16,128]{4,3,1,0,2:T(8,128)S(1)} %copy.84), channel_id=1, replica_groups=mesh['space'=32,'modes'=16] {'modes'}, dimensions={2} | all-to-all | bytes 2097152 | tf_op jit(solution)/shard_map/all_to_all | solution.py:148
  158.2 0.7 copy.85
  158.9 1.4 reshape.98
  (79 shorter events, 3.6 us)
Async XLA Ops:
  0.0 28.4 %copy-start.2 = (bf16[2,16,16,512]{3,2,1,0:T(8,128)(2,1)S(1)}, bf16[2,16,16,512]{3,2,1,0:T(8,128)(2,1)}, u32[]{:S(2)}) copy-start(bf16[2,16,16,512]{3,2,1,0:T(8,128)(2,1)} %param.8) | copy-start | bytes 1572868
  1.2 27.3 %collective-permute-start = (bf16[2,1,16,512]{3,1,2,0:T(2,128)(2,1)S(1)}, bf16[2,1,16,512]{3,1,2,0:T(2,128)(2,1)S(1)}, u32[]{:S(2)}, u32[]{:S(2)}) collective-permute-start(bf16[2,1,16,512]{3,1,2,0:T(2,128)(2,1)S(1)} %get-tuple-element.25), channel_id=1, source_target_pairs={{0,16},{16,32},{32,48},{48,64},{64,80},{80,96},{96,112},{112,128},... | collective-permute-start | bytes 98312 | tf_op jit(solution)/shard_map/ppermute | solution.py:14
  4.9 23.6 %collective-permute-start.1 = (bf16[2,1,16,512]{3,1,2,0:T(2,128)(2,1)S(1)}, bf16[2,1,16,512]{3,1,2,0:T(2,128)(2,1)S(1)}, u32[]{:S(2)}, u32[]{:S(2)}) collective-permute-start(bf16[2,1,16,512]{3,1,2,0:T(2,128)(2,1)S(1)} %get-tuple-element.26), channel_id=1, source_target_pairs={{16,0},{32,16},{48,32},{64,48},{80,64},{96,80},{112,96},{128,112},... | collective-permute-start | bytes 98312 | tf_op jit(solution)/shard_map/ppermute | solution.py:15
  8.2 27.0 %all-to-all-start.1 = ((f32[16,1,256]{2,1,0:T(1,128)}), f32[16,1,256]{2,1,0:T(1,128)S(1)}, u32[]{:S(2)}, u32[]{:S(2)}) async-start(f32[16,1,256]{2,1,0:T(1,128)} %reshape.115), calls=%async_computation.1 | async-start | bytes 32768 | tf_op jit(solution)/shard_map/all_to_all | solution.py:55
  24.9 3.6 %copy-start = (bf16[2,16,16,512]{3,2,1,0:T(8,128)(2,1)S(1)}, bf16[2,16,16,512]{3,2,1,0:T(8,128)(2,1)}, u32[]{:S(2)}) copy-start(bf16[2,16,16,512]{3,2,1,0:T(8,128)(2,1)} %param.9) | copy-start | bytes 1572868
  35.3 9.3 %copy-start.7 = (s32[3,16,16]{2,1,0:T(8,128)S(1)}, s32[3,16,16]{2,1,0:T(8,128)}, u32[]{:S(2)}) copy-start(s32[3,16,16]{2,1,0:T(8,128)} %param.14) | copy-start | bytes 9220
  35.3 9.3 %copy-start.4 = (f32[2,3,8]{2,0,1:T(2,128)S(1)}, f32[2,3,8]{2,0,1:T(2,128)}, u32[]{:S(2)}) copy-start(f32[2,3,8]{2,0,1:T(2,128)} %param.12) | copy-start | bytes 580
  35.3 10.2 %copy-start.6 = (s32[16,512]{1,0:T(8,128)S(1)}, s32[16,512]{1,0:T(8,128)}, u32[]{:S(2)}) copy-start(s32[16,512]{1,0:T(8,128)} %param.10) | copy-start | bytes 98308
  35.3 43.6 %all-to-all-start = ((bf16[16,2,11,16,128]{4,3,2,1,0:T(8,128)(2,1)}), bf16[16,2,11,16,128]{4,3,2,1,0:T(8,128)(2,1)}, u32[]{:S(2)}, u32[]{:S(2)}) async-start(bf16[16,2,11,16,128]{4,3,2,1,0:T(8,128)(2,1)} %bitcast.8), calls=%async_computation | async-start | bytes 2883584 | tf_op jit(solution)/shard_map/all_to_all | solution.py:111
  46.4 3.7 %copy-start.5 = (f32[2,8]{1,0:T(2,128)S(1)}, f32[2,8]{1,0:T(2,128)}, u32[]{:S(2)}) copy-start(f32[2,8]{1,0:T(2,128)} %param.11) | copy-start | bytes 196
  84.6 1.6 %copy-start.3 = (bf16[3,256,256]{2,1,0:T(8,128)(2,1)S(1)}, bf16[3,256,256]{2,1,0:T(8,128)(2,1)}, u32[]{:S(2)}) copy-start(bf16[3,256,256]{2,1,0:T(8,128)(2,1)} %mul.429) | copy-start | bytes 1179652
  84.6 1.6 %copy-start.8 = (f32[2,4,128]{2,1,0:T(4,128)S(1)}, f32[2,4,128]{2,1,0:T(4,128)}, u32[]{:S(2)}) copy-start(f32[2,4,128]{2,1,0:T(4,128)} %get-tuple-element.13) | copy-start | bytes 12292
  84.6 1.6 %copy-start.9 = (f32[2,4,128]{2,1,0:T(4,128)S(1)}, f32[2,4,128]{2,1,0:T(4,128)}, u32[]{:S(2)}) copy-start(f32[2,4,128]{2,1,0:T(4,128)} %get-tuple-element.14) | copy-start | bytes 12292
  84.6 1.6 %copy-start.10 = (bf16[3,256,256]{2,1,0:T(8,128)(2,1)S(1)}, bf16[3,256,256]{2,1,0:T(8,128)(2,1)}, u32[]{:S(2)}) copy-start(bf16[3,256,256]{2,1,0:T(8,128)(2,1)} %param.13) | copy-start | bytes 1179652
  86.2 1.0 copy-start.1
  88.4 17.5 %collective-permute-start.4 = (f32[2,4,256]{2,1,0:T(4,128)S(1)}, f32[2,4,256]{2,1,0:T(4,128)S(1)}, u32[]{:S(2)}, u32[]{:S(2)}) collective-permute-start(f32[2,4,256]{2,1,0:T(4,128)S(1)} %bitcast.146), channel_id=1, source_target_pairs={{1,0},{2,1},{3,2},{5,4},{6,5},{7,6},{9,8},{10,9},{11,10},{13,12},{... | collective-permute-start | bytes 24584 | tf_op jit(solution)/shard_map/ppermute | solution.py:125
  89.8 16.2 %collective-permute-start.5 = (f32[2,4,256]{2,1,0:T(4,128)S(1)}, f32[2,4,256]{2,1,0:T(4,128)S(1)}, u32[]{:S(2)}, u32[]{:S(2)}) collective-permute-start(f32[2,4,256]{2,1,0:T(4,128)S(1)} %bitcast.147), channel_id=1, source_target_pairs={{0,1},{1,2},{2,3},{4,5},{5,6},{6,7},{8,9},{9,10},{10,11},{12,13},{... | collective-permute-start | bytes 24584 | tf_op jit(solution)/shard_map/ppermute | solution.py:124
  95.3 18.0 %collective-permute-start.3 = (f32[2,1,256,128]{2,3,1,0:T(8,128)S(1)}, f32[2,1,256,128]{2,3,1,0:T(8,128)S(1)}, u32[]{:S(2)}, u32[]{:S(2)}) collective-permute-start(f32[2,1,256,128]{2,3,1,0:T(8,128)S(1)} %get-tuple-element.21), channel_id=1, source_target_pairs={{0,4},{1,5},{2,6},{3,7},{4,8},{5,9},{6,10},{7,11},{8,12},{9,13},{1... | collective-permute-start | bytes 786440 | tf_op jit(solution)/shard_map/ppermute | solution.py:122
  99.8 13.6 %collective-permute-start.2 = (f32[2,1,256,128]{2,3,1,0:T(8,128)S(1)}, f32[2,1,256,128]{2,3,1,0:T(8,128)S(1)}, u32[]{:S(2)}, u32[]{:S(2)}) collective-permute-start(f32[2,1,256,128]{2,3,1,0:T(8,128)S(1)} %get-tuple-element.22), channel_id=1, source_target_pairs={{4,0},{5,1},{6,2},{7,3},{8,4},{9,5},{10,6},{11,7},{12,8},{13,9},{1... | collective-permute-start | bytes 786440 | tf_op jit(solution)/shard_map/ppermute | solution.py:123

commit v5 on v4

--- a/solution.py
+++ b/solution.py
@@ -52,12 +52,11 @@
     my_r = me // col_chunks
     my_c = me % col_chunks
 
-    every = lax.all_to_all(
-        jnp.broadcast_to(block_inverse, (devs,) + block_inverse.shape[1:]),
-        "modes", split_axis=0, concat_axis=0, tiled=True,
-    )
-    eye = jnp.eye(blocks, dtype=jnp.float32)
-    dense_inv = (every[:, :, None, :] * eye[:, None, :, None]).reshape(modes_all, modes_all)
+    inv_hi = lax.optimization_barrier(block_inverse[0].astype(jnp.bfloat16))
+    rest = block_inverse[0] - inv_hi.astype(jnp.float32)
+    inv_mid = lax.optimization_barrier(rest.astype(jnp.bfloat16))
+    inv_lo = (rest - inv_mid.astype(jnp.float32)).astype(jnp.bfloat16)
+    inv_code = jnp.concatenate([inv_hi, inv_mid, inv_lo], axis=-1)
 
     base = lax.dynamic_slice(
         lookup(base_table, region), (0, my_r * rows_c, my_c * LANES), (fields, rows_c, LANES)
@@ -69,6 +68,11 @@
     )
     coef = coef.transpose(0, 2, 1, 3)[:, :, :, None, :]
     inverse_base = 1.0 / (4.0 * base)
+
+    rp = rhs.reshape(fields, modes_dev, row_chunks, rows_c, col_chunks, LANES)
+    rp = rp.transpose(2, 4, 0, 3, 1, 5).reshape(devs, fields, rows_c, modes_dev, LANES)
+    rhs_c = lax.all_to_all(rp, "modes", split_axis=0, concat_axis=3, tiled=True)[0]
+    rhs_c = rhs_c.astype(jnp.float32)
 
     init_x = ring_halo(initial.transpose(0, 2, 1, 3), "space", 1)
 
@@ -102,11 +106,12 @@
         for h in (hl, hr):
             h = h.reshape(fields, row_chunks, rows_c, modes_dev, col_chunks)
             sides.append(h.transpose(0, 1, 3, 4, 2))
-        side = jnp.concatenate(sides, axis=-1)
-        side = jnp.pad(side, ((0, 0),) * 4 + ((0, LANES - 2 * rows_c),))[:, :, None]
-        rp = rhs_f.reshape(fields, modes_dev, row_chunks, rows_c, col_chunks, LANES)
-        rp = rp.transpose(0, 2, 3, 1, 4, 5)
-        full = jnp.concatenate([main, side, rp], axis=2)
+        code = jnp.broadcast_to(
+            inv_code[None, None, :, None, :], sides[0].shape[:-1] + inv_code.shape[-1:]
+        )
+        side = jnp.concatenate(sides + [code], axis=-1)
+        side = jnp.pad(side, ((0, 0),) * 4 + ((0, LANES - side.shape[-1]),))[:, :, None]
+        full = jnp.concatenate([main, side], axis=2)
         full = full.transpose(1, 4, 0, 2, 3, 5).reshape(devs, fields, -1, modes_dev, LANES)
         return lax.all_to_all(full, "modes", split_axis=0, concat_axis=3, tiled=True)[0]
 
@@ -115,7 +120,11 @@
     side = got[:, rows_c + 2].astype(jnp.float32)
     fill_l = side[..., :rows_c].transpose(0, 2, 1)
     fill_r = side[..., rows_c : 2 * rows_c].transpose(0, 2, 1)
-    rhs_c = got[:, rows_c + 3 :].astype(jnp.float32)
+    code = side[0, :, 2 * rows_c : 2 * rows_c + 3 * width]
+    every = (code[:, :width] + code[:, width : 2 * width]) + code[:, 2 * width :]
+    every = every.reshape(blocks, width, width)
+    eye = jnp.eye(blocks, dtype=jnp.float32)
+    dense_inv = (every[:, :, None, :] * eye[:, None, :, None]).reshape(modes_all, modes_all)
     u_field = padded[:, 1:-1]
     for sweep in range(SWEEPS):
         if sweep > 0:
@@ -127,11 +136,10 @@
         lap = laplace_rows(padded, fill_l, fill_r)
         local = base * lap
         if sweep > 0:
-            lap_r = laplace_rows(
-                padded.astype(jnp.bfloat16).astype(jnp.float32),
-                fill_l.astype(jnp.bfloat16).astype(jnp.float32),
-                fill_r.astype(jnp.bfloat16).astype(jnp.float32),
+            rounded = lax.optimization_barrier(
+                (padded.astype(jnp.bfloat16), fill_l.astype(jnp.bfloat16), fill_r.astype(jnp.bfloat16))
             )
+            lap_r = laplace_rows(*(part.astype(jnp.float32) for part in rounded))
         else:
             lap_r = lap
         tiles = (coef * lap_r[:, :, None]).astype(jnp.bfloat16)

time: 161 us -> 151 us (0.938)
  the two profiles are of different devices: /device:TPU:25 before, /device:TPU:26 now
where the time goes in v5:
time: 151 us; the launch traced here: 150 us
  waiting for transfers between devices  41.4 us (27%)
  blocking collectives  37.4 us (25%)
  starting transfers between devices  34.7 us (23%)
  local copies, waits for them, and re-layouts  24.6 us (16%)
  other arithmetic  7.21 us (5%)
  matrix products  4.03 us (3%)
    all_to_all x1, blocking collectives, body(): back = lax.all_to_all(out, 'modes', split_axis=2, concat_axis=2, tiled=True)  37.4 us
    all_to_all x1, waiting for transfers between devices, pack(): lax.all_to_all(full, 'modes', split_axis=0, concat_axis=3, tiled=True)[0]  18.3 us
    all_to_all x1, waiting for transfers between devices, body(): lax.all_to_all(rp, 'modes', split_axis=0, concat_axis=3, tiled=True)[0]  12 us
    all_to_all x1, starting transfers between devices, body(): lax.all_to_all(rp, 'modes', split_axis=0, concat_axis=3, tiled=True)[0]  12 us
    ppermute x1, waiting for transfers between devices, body(): low = lax.ppermute(u_field[:, -1:], flat, down)  5.78 us
    ppermute x1, waiting for transfers between devices, body(): high = lax.ppermute(u_field[:, :1], flat, up)  5.25 us
    ppermute x1, starting transfers between devices, body(): high = lax.ppermute(u_field[:, :1], flat, up)  5.08 us
    all_to_all x1, starting transfers between devices, pack(): lax.all_to_all(full, 'modes', split_axis=0, concat_axis=3, tiled=True)[0]  4.32 us
  transfers between devices with their start and end apart: 8, of which 4 were waited for; matrix products, arithmetic and copies ran while one was open for 12% of the time, Pallas kernels for 0%

profile of v5, /device:TPU:26, one launch (start us, length us, event | category | flops | bytes accessed | tf_op | source)
XLA Modules:
  0.0 150.0 jit_solution(7329930796363519525)
XLA Ops:
  0.0 1.1 fusion.63
  1.1 1.9 %collective-permute-start = (bf16[2,1,16,512]{3,1,2,0:T(2,128)(2,1)S(1)}, bf16[2,1,16,512]{3,1,2,0:T(2,128)(2,1)S(1)}, u32[]{:S(2)}, u32[]{:S(2)}) collective-permute-start(bf16[2,1,16,512]{3,1,2,0:T(2,128)(2,1)S(1)} %get-tuple-element.31), channel_id=1, source_target_pairs={{0,16},{16,32},{32,48},{48,64},{64,80},{80,96},{96,112},{112,128},... | collective-permute-start | bytes 98312 | tf_op jit(solution)/shard_map/ppermute | solution.py:14
  3.1 3.8 %collective-permute-start.1 = (bf16[2,1,16,512]{3,1,2,0:T(2,128)(2,1)S(1)}, bf16[2,1,16,512]{3,1,2,0:T(2,128)(2,1)S(1)}, u32[]{:S(2)}, u32[]{:S(2)}) collective-permute-start(bf16[2,1,16,512]{3,1,2,0:T(2,128)(2,1)S(1)} %get-tuple-element.32), channel_id=1, source_target_pairs={{16,0},{32,16},{48,32},{64,48},{80,64},{96,80},{112,96},{128,112},... | collective-permute-start | bytes 98312 | tf_op jit(solution)/shard_map/ppermute | solution.py:15
  6.9 1.2 reshape.104
  8.0 1.1 copy.70
  9.2 12.0 %all-to-all-start.1 = ((bf16[16,2,4,16,128]{4,3,2,1,0:T(8,128)(2,1)}), bf16[16,2,4,16,128]{4,3,2,1,0:T(8,128)(2,1)S(1)}, u32[]{:S(2)}, u32[]{:S(2)}) async-start(bf16[16,2,4,16,128]{4,3,2,1,0:T(8,128)(2,1)} %bitcast.13), calls=%async_computation.1 | async-start | bytes 1048576 | tf_op jit(solution)/shard_map/all_to_all | solution.py:74
  21.2 0.5 slice.155
  21.7 0.5 slice.156
  22.4 1.0 copy.63
  23.5 1.0 copy.64
  24.6 0.1 fusion.43
  24.9 0.3 copy.66
  25.3 0.4 pad_maximum_fusion.3
  25.7 0.8 slice.154
  26.5 0.8 slice.153
  27.5 1.1 pad_maximum_fusion.2
  28.5 12.0 %all-to-all-done.1 = bf16[16,2,4,16,128]{4,3,2,1,0:T(8,128)(2,1)S(1)} async-done(((bf16[16,2,4,16,128]{4,3,2,1,0:T(8,128)(2,1)}), bf16[16,2,4,16,128]{4,3,2,1,0:T(8,128)(2,1)S(1)}, u32[]{:S(2)}, u32[]{:S(2)}) %all-to-all-start.1) | async-done | bytes 524320 | tf_op jit(solution)/shard_map/all_to_all | solution.py:74
  40.6 4.3 %all-to-all-start = ((bf16[16,2,7,16,128]{4,3,2,1,0:T(8,128)(2,1)}), bf16[16,2,7,16,128]{4,3,2,1,0:T(8,128)(2,1)}, u32[]{:S(2)}, u32[]{:S(2)}) async-start(bf16[16,2,7,16,128]{4,3,2,1,0:T(8,128)(2,1)} %bitcast.8), calls=%async_computation | async-start | bytes 1835008 | tf_op jit(solution)/shard_map/all_to_all | solution.py:116
  46.3 0.5 mul.430
  46.8 3.7 %mul.431 = bf16[3,256,256]{2,1,0:T(8,128)(2,1)} reshape(bf16[3,16,16,16,16]{4,3,2,1,0:T(8,128)(2,1)S(1)} %mul.430) | data formatting | bytes 786432 | tf_op jit(solution)/shard_map/mul | solution.py:39
  50.5 0.3 slice_reduce_fusion.4
  50.9 0.2 multiply_add_fusion
  51.2 1.1 bitcast_convert_fusion
  52.3 1.3 copy.74
  53.7 18.3 %all-to-all-done = bf16[16,2,7,16,128]{4,3,2,1,0:T(8,128)(2,1)} async-done(((bf16[16,2,7,16,128]{4,3,2,1,0:T(8,128)(2,1)}), bf16[16,2,7,16,128]{4,3,2,1,0:T(8,128)(2,1)}, u32[]{:S(2)}, u32[]{:S(2)}) %all-to-all-start) | async-done | bytes 917536 | tf_op jit(solution)/shard_map/all_to_all | solution.py:116
  72.0 1.4 copy.68
  73.6 0.3 copy.97
  74.1 1.2 fusion.62
  75.4 1.5 %broadcast_multiply_fusion = f32[16,16,16,16]{3,2,1,0:T(8,128)} fusion(f32[16,16]{1,0:T(8,128)S(1)} %fusion.50, f32[16,16,16]{2,1,0:T(8,128)S(1)} %bitcast.153), kind=kLoop, calls=%fused_computation.43 | loop fusion | flops 65536 | bytes 279552 | tf_op jit(solution)/shard_map/mul | solution.py:127
  76.9 2.4 %reshape.116 = f32[256,256,1,1]{1,0,2,3:T(8,128)S(1)} reshape(f32[16,16,16,16]{3,2,1,0:T(8,128)} %broadcast_multiply_fusion) | data formatting | bytes 524288 | tf_op jit(solution)/shard_map/mul | solution.py:127
  79.4 1.6 %fusion.31 = f32[2,4,256,128]{2,3,1,0:T(8,128)S(1)} fusion(f32[2,6,256,128]{2,3,1,0:T(8,128)S(1)} %convert_element_type.128, f32[2,4,256,1]{2,3,1,0:T(1,128)S(1)} %broadcast_in_dim.24, f32[2,4,256,127]{2,3,1,0:T(8,128)} %get-tuple-element.30, f32[2,4,256,127]{2,3,1,0:T(8,128)S(1)} %get-tuple-element.29, f32[2,4,256,1]{2,3,1,0:T(1,128)S(1)} %copy.73), kind=kLoop, calls=%fused_computation.41 | loop fusion | flops 1835008 | bytes 6291456 | tf_op jit(solution)/shard_map/sub | solution.py:30
  81.1 0.9 fusion.16
  82.0 1.1 fusion.65
  83.1 2.6 %collective-permute-start.5 = (f32[2,4,256]{2,1,0:T(4,128)S(1)}, f32[2,4,256]{2,1,0:T(4,128)S(1)}, u32[]{:S(2)}, u32[]{:S(2)}) collective-permute-start(f32[2,4,256]{2,1,0:T(4,128)S(1)} %bitcast.161), channel_id=1, source_target_pairs={{0,1},{1,2},{2,3},{4,5},{5,6},{6,7},{8,9},{9,10},{10,11},{12,13},{... | collective-permute-start | bytes 24584 | tf_op jit(solution)/shard_map/ppermute | solution.py:133
  85.8 1.3 collective-permute-start.4
  87.1 3.7 %collective-permute-start.3 = (f32[2,1,256,128]{2,3,1,0:T(8,128)S(1)}, f32[2,1,256,128]{2,3,1,0:T(8,128)S(1)}, u32[]{:S(2)}, u32[]{:S(2)}) collective-permute-start(f32[2,1,256,128]{2,3,1,0:T(8,128)S(1)} %get-tuple-element.25), channel_id=1, source_target_pairs={{0,4},{1,5},{2,6},{3,7},{4,8},{5,9},{6,10},{7,11},{8,12},{9,13},{1... | collective-permute-start | bytes 786440 | tf_op jit(solution)/shard_map/ppermute | solution.py:131
  90.7 5.1 %collective-permute-start.2 = (f32[2,1,256,128]{2,3,1,0:T(8,128)S(1)}, f32[2,1,256,128]{2,3,1,0:T(8,128)S(1)}, u32[]{:S(2)}, u32[]{:S(2)}) collective-permute-start(f32[2,1,256,128]{2,3,1,0:T(8,128)S(1)} %get-tuple-element.26), channel_id=1, source_target_pairs={{4,0},{5,1},{6,2},{7,3},{8,4},{9,5},{10,6},{11,7},{12,8},{13,9},{1... | collective-permute-start | bytes 786440 | tf_op jit(solution)/shard_map/ppermute | solution.py:132
  95.8 0.2 fusion.58
  96.1 5.8 %collective-permute-done.3 = f32[2,1,256,128]{2,3,1,0:T(8,128)S(1)} collective-permute-done((f32[2,1,256,128]{2,3,1,0:T(8,128)S(1)}, f32[2,1,256,128]{2,3,1,0:T(8,128)S(1)}, u32[]{:S(2)}, u32[]{:S(2)}) %collective-permute-start.3) | collective-permute-done | bytes 262176 | tf_op jit(solution)/shard_map/ppermute | solution.py:131
  101.9 5.3 %collective-permute-done.2 = f32[2,1,256,128]{2,3,1,0:T(8,128)S(1)} collective-permute-done((f32[2,1,256,128]{2,3,1,0:T(8,128)S(1)}, f32[2,1,256,128]{2,3,1,0:T(8,128)S(1)}, u32[]{:S(2)}, u32[]{:S(2)}) %collective-permute-start.2) | collective-permute-done | bytes 262176 | tf_op jit(solution)/shard_map/ppermute | solution.py:132
  107.4 0.2 fusion.61
  107.7 0.3 fusion.23
  107.9 1.1 fusion.21
  109.0 1.0 fusion.9
  110.1 0.3 copy.89
  110.5 37.4 %all_to_all.29 = f32[2,4,16,16,128]{4,3,1,0,2:T(8,128)S(1)} all-to-all(f32[2,4,16,16,128]{4,3,1,0,2:T(8,128)S(1)} %copy.90), channel_id=1, replica_groups=mesh['space'=32,'modes'=16] {'modes'}, dimensions={2} | all-to-all | bytes 2097152 | tf_op jit(solution)/shard_map/all_to_all | solution.py:156
  147.9 0.7 copy.91
  148.6 1.4 reshape.108
  (82 shorter events, 3.2 us)
Async XLA Ops:
  1.1 24.1 %collective-permute-start = (bf16[2,1,16,512]{3,1,2,0:T(2,128)(2,1)S(1)}, bf16[2,1,16,512]{3,1,2,0:T(2,128)(2,1)S(1)}, u32[]{:S(2)}, u32[]{:S(2)}) collective-permute-start(bf16[2,1,16,512]{3,1,2,0:T(2,128)(2,1)S(1)} %get-tuple-element.31), channel_id=1, source_target_pairs={{0,16},{16,32},{32,48},{48,64},{64,80},{80,96},{96,112},{112,128},... | collective-permute-start | bytes 98312 | tf_op jit(solution)/shard_map/ppermute | solution.py:14
  3.1 18.1 %copy-start.5 = (f32[1,16,16]{2,1,0:T(8,128)S(1)}, f32[1,16,16]{2,1,0:T(8,128)}, u32[]{:S(2)}) copy-start(f32[1,16,16]{2,1,0:T(8,128)} %param.15) | copy-start | bytes 3076
  3.1 18.1 %copy-start = (bf16[2,16,16,512]{3,2,1,0:T(8,128)(2,1)S(1)}, bf16[2,16,16,512]{3,2,1,0:T(8,128)(2,1)}, u32[]{:S(2)}) copy-start(bf16[2,16,16,512]{3,2,1,0:T(8,128)(2,1)} %param.9) | copy-start | bytes 1572868
  3.1 22.2 %collective-permute-start.1 = (bf16[2,1,16,512]{3,1,2,0:T(2,128)(2,1)S(1)}, bf16[2,1,16,512]{3,1,2,0:T(2,128)(2,1)S(1)}, u32[]{:S(2)}, u32[]{:S(2)}) collective-permute-start(bf16[2,1,16,512]{3,1,2,0:T(2,128)(2,1)S(1)} %get-tuple-element.32), channel_id=1, source_target_pairs={{16,0},{32,16},{48,32},{64,48},{80,64},{96,80},{112,96},{128,112},... | collective-permute-start | bytes 98312 | tf_op jit(solution)/shard_map/ppermute | solution.py:15
  9.2 31.4 %all-to-all-start.1 = ((bf16[16,2,4,16,128]{4,3,2,1,0:T(8,128)(2,1)}), bf16[16,2,4,16,128]{4,3,2,1,0:T(8,128)(2,1)S(1)}, u32[]{:S(2)}, u32[]{:S(2)}) async-start(bf16[16,2,4,16,128]{4,3,2,1,0:T(8,128)(2,1)} %bitcast.13), calls=%async_computation.1 | async-start | bytes 1048576 | tf_op jit(solution)/shard_map/all_to_all | solution.py:74
  27.5 17.5 %copy-start.4 = (f32[2,3,8]{2,0,1:T(2,128)S(1)}, f32[2,3,8]{2,0,1:T(2,128)}, u32[]{:S(2)}) copy-start(f32[2,3,8]{2,0,1:T(2,128)} %param.12) | copy-start | bytes 580
  27.5 17.6 %copy-start.8 = (s32[3,16,16]{2,1,0:T(8,128)S(1)}, s32[3,16,16]{2,1,0:T(8,128)}, u32[]{:S(2)}) copy-start(s32[3,16,16]{2,1,0:T(8,128)} %param.14) | copy-start | bytes 9220
  27.5 18.4 %copy-start.7 = (s32[16,512]{1,0:T(8,128)S(1)}, s32[16,512]{1,0:T(8,128)}, u32[]{:S(2)}) copy-start(s32[16,512]{1,0:T(8,128)} %param.10) | copy-start | bytes 98308
  40.6 5.6 %copy-start.1 = (bf16[16,2,4,16,128]{4,3,2,1,0:T(8,128)(2,1)}, bf16[16,2,4,16,128]{4,3,2,1,0:T(8,128)(2,1)S(1)}, u32[]{:S(2)}) copy-start(bf16[16,2,4,16,128]{4,3,2,1,0:T(8,128)(2,1)S(1)} %all-to-all-done.1) | copy-start | bytes 1572868
  40.6 31.4 %all-to-all-start = ((bf16[16,2,7,16,128]{4,3,2,1,0:T(8,128)(2,1)}), bf16[16,2,7,16,128]{4,3,2,1,0:T(8,128)(2,1)}, u32[]{:S(2)}, u32[]{:S(2)}) async-start(bf16[16,2,7,16,128]{4,3,2,1,0:T(8,128)(2,1)} %bitcast.8), calls=%async_computation | async-start | bytes 1835008 | tf_op jit(solution)/shard_map/all_to_all | solution.py:116
  46.7 3.7 %copy-start.6 = (f32[2,8]{1,0:T(2,128)S(1)}, f32[2,8]{1,0:T(2,128)}, u32[]{:S(2)}) copy-start(f32[2,8]{1,0:T(2,128)} %param.11) | copy-start | bytes 196
  79.4 1.7 %copy-start.2 = (f32[2,4,256,128]{2,3,1,0:T(8,128)S(1)}, f32[2,4,256,128]{2,3,1,0:T(8,128)}, u32[]{:S(2)}) copy-start(f32[2,4,256,128]{2,3,1,0:T(8,128)} %copy.74) | copy-start | bytes 3145732
  79.4 1.7 %copy-start.3 = (bf16[3,256,256]{2,1,0:T(8,128)(2,1)S(1)}, bf16[3,256,256]{2,1,0:T(8,128)(2,1)}, u32[]{:S(2)}) copy-start(bf16[3,256,256]{2,1,0:T(8,128)(2,1)} %mul.431) | copy-start | bytes 1179652
  79.4 1.7 %copy-start.9 = (bf16[3,256,256]{2,1,0:T(8,128)(2,1)S(1)}, bf16[3,256,256]{2,1,0:T(8,128)(2,1)}, u32[]{:S(2)}) copy-start(bf16[3,256,256]{2,1,0:T(8,128)(2,1)} %param.13) | copy-start | bytes 1179652
  83.1 12.9 %collective-permute-start.5 = (f32[2,4,256]{2,1,0:T(4,128)S(1)}, f32[2,4,256]{2,1,0:T(4,128)S(1)}, u32[]{:S(2)}, u32[]{:S(2)}) collective-permute-start(f32[2,4,256]{2,1,0:T(4,128)S(1)} %bitcast.161), channel_id=1, source_target_pairs={{0,1},{1,2},{2,3},{4,5},{5,6},{6,7},{8,9},{9,10},{10,11},{12,13},{... | collective-permute-start | bytes 24584 | tf_op jit(solution)/shard_map/ppermute | solution.py:133
  85.8 10.3 %collective-permute-start.4 = (f32[2,4,256]{2,1,0:T(4,128)S(1)}, f32[2,4,256]{2,1,0:T(4,128)S(1)}, u32[]{:S(2)}, u32[]{:S(2)}) collective-permute-start(f32[2,4,256]{2,1,0:T(4,128)S(1)} %bitcast.160), channel_id=1, source_target_pairs={{1,0},{2,1},{3,2},{5,4},{6,5},{7,6},{9,8},{10,9},{11,10},{13,12},{... | collective-permute-start | bytes 24584 | tf_op jit(solution)/shard_map/ppermute | solution.py:134
  87.1 14.8 %collective-permute-start.3 = (f32[2,1,256,128]{2,3,1,0:T(8,128)S(1)}, f32[2,1,256,128]{2,3,1,0:T(8,128)S(1)}, u32[]{:S(2)}, u32[]{:S(2)}) collective-permute-start(f32[2,1,256,128]{2,3,1,0:T(8,128)S(1)} %get-tuple-element.25), channel_id=1, source_target_pairs={{0,4},{1,5},{2,6},{3,7},{4,8},{5,9},{6,10},{7,11},{8,12},{9,13},{1... | collective-permute-start | bytes 786440 | tf_op jit(solution)/shard_map/ppermute | solution.py:131
  90.7 16.4 %collective-permute-start.2 = (f32[2,1,256,128]{2,3,1,0:T(8,128)S(1)}, f32[2,1,256,128]{2,3,1,0:T(8,128)S(1)}, u32[]{:S(2)}, u32[]{:S(2)}) collective-permute-start(f32[2,1,256,128]{2,3,1,0:T(8,128)S(1)} %get-tuple-element.26), channel_id=1, source_target_pairs={{4,0},{5,1},{6,2},{7,3},{8,4},{9,5},{10,6},{11,7},{12,8},{13,9},{1... | collective-permute-start | bytes 786440 | tf_op jit(solution)/shard_map/ppermute | solution.py:132

commit v6 on v5

--- a/solution.py
+++ b/solution.py
@@ -30,7 +30,7 @@
     return 4.0 * center - padded[:, 2:] - padded[:, :-2] - right - left
 
 
-def body(rhs, initial, region, base_table, term_table, galerkin, block_mask, block_inverse):
+def sweeps(rhs, initial, region, base_table, term_table, galerkin, block_mask, block_inverse):
     terms = galerkin.shape[0]
     modes_all = galerkin.shape[1]
     blocks = block_mask.shape[1]
@@ -93,7 +93,7 @@
     ]
     leftward = [(b, a) for a, b in rightward]
 
-    def pack(init_f, rhs_f):
+    def pack(init_f):
         top = init_f[:, 0 : rows : rows_c]
         mid = init_f[:, 1 : rows + 1].reshape(fields, row_chunks, rows_c, modes_dev, cols)
         bot = init_f[:, rows_c + 1 : rows + 2 : rows_c]
@@ -115,7 +115,7 @@
         full = full.transpose(1, 4, 0, 2, 3, 5).reshape(devs, fields, -1, modes_dev, LANES)
         return lax.all_to_all(full, "modes", split_axis=0, concat_axis=3, tiled=True)[0]
 
-    got = pack(init_x, rhs)
+    got = pack(init_x)
     padded = got[:, : rows_c + 2].astype(jnp.float32)
     side = got[:, rows_c + 2].astype(jnp.float32)
     fill_l = side[..., :rows_c].transpose(0, 2, 1)
@@ -170,4 +170,4 @@
         P("modes", None, None),
     )
     out_specs = P(None, "modes", "space", None)
-    return jax.shard_map(body, mesh=mesh, in_specs=in_specs, out_specs=out_specs, check_vma=False)
+    return jax.shard_map(sweeps, mesh=mesh, in_specs=in_specs, out_specs=out_specs, check_vma=False)

time: 151 us -> 151 us (level)
  no operation moved by 1% of the time
where the time goes in v6:
time: 151 us; the launch traced here: 150 us
  waiting for transfers between devices  41.4 us (27%)
  blocking collectives  37.4 us (25%)
  starting transfers between devices  34.7 us (23%)
  local copies, waits for them, and re-layouts  24.6 us (16%)
  other arithmetic  7.21 us (5%)
  matrix products  4.03 us (3%)
    all_to_all x1, blocking collectives, sweeps(): back = lax.all_to_all(out, 'modes', split_axis=2, concat_axis=2, tiled=True)  37.4 us
    all_to_all x1, waiting for transfers between devices, pack(): lax.all_to_all(full, 'modes', split_axis=0, concat_axis=3, tiled=True)[0]  18.3 us
    all_to_all x1, waiting for transfers between devices, sweeps(): lax.all_to_all(rp, 'modes', split_axis=0, concat_axis=3, tiled=True)[0]  12 us
    all_to_all x1, starting transfers between devices, sweeps(): lax.all_to_all(rp, 'modes', split_axis=0, concat_axis=3, tiled=True)[0]  12 us
    ppermute x1, waiting for transfers between devices, sweeps(): low = lax.ppermute(u_field[:, -1:], flat, down)  5.78 us
    ppermute x1, waiting for transfers between devices, sweeps(): high = lax.ppermute(u_field[:, :1], flat, up)  5.25 us
    ppermute x1, starting transfers between devices, sweeps(): high = lax.ppermute(u_field[:, :1], flat, up)  5.08 us
    all_to_all x1, starting transfers between devices, pack(): lax.all_to_all(full, 'modes', split_axis=0, concat_axis=3, tiled=True)[0]  4.32 us
  transfers between devices with their start and end apart: 8, of which 4 were waited for; matrix products, arithmetic and copies ran while one was open for 12% of the time, Pallas kernels for 0%

profile of v6, /device:TPU:26, one launch (start us, length us, event | category | flops | bytes accessed | tf_op | source)
XLA Modules:
  0.0 150.0 jit_solution(7329930796363519525)
XLA Ops:
  0.0 1.1 fusion.63
  1.1 1.9 %collective-permute-start = (bf16[2,1,16,512]{3,1,2,0:T(2,128)(2,1)S(1)}, bf16[2,1,16,512]{3,1,2,0:T(2,128)(2,1)S(1)}, u32[]{:S(2)}, u32[]{:S(2)}) collective-permute-start(bf16[2,1,16,512]{3,1,2,0:T(2,128)(2,1)S(1)} %get-tuple-element.31), channel_id=1, source_target_pairs={{0,16},{16,32},{32,48},{48,64},{64,80},{80,96},{96,112},{112,128},... | collective-permute-start | bytes 98312 | tf_op jit(solution)/shard_map/ppermute | solution.py:14
  3.1 3.8 %collective-permute-start.1 = (bf16[2,1,16,512]{3,1,2,0:T(2,128)(2,1)S(1)}, bf16[2,1,16,512]{3,1,2,0:T(2,128)(2,1)S(1)}, u32[]{:S(2)}, u32[]{:S(2)}) collective-permute-start(bf16[2,1,16,512]{3,1,2,0:T(2,128)(2,1)S(1)} %get-tuple-element.32), channel_id=1, source_target_pairs={{16,0},{32,16},{48,32},{64,48},{80,64},{96,80},{112,96},{128,112},... | collective-permute-start | bytes 98312 | tf_op jit(solution)/shard_map/ppermute | solution.py:15
  6.9 1.2 reshape.104
  8.0 1.1 copy.70
  9.2 12.0 %all-to-all-start.1 = ((bf16[16,2,4,16,128]{4,3,2,1,0:T(8,128)(2,1)}), bf16[16,2,4,16,128]{4,3,2,1,0:T(8,128)(2,1)S(1)}, u32[]{:S(2)}, u32[]{:S(2)}) async-start(bf16[16,2,4,16,128]{4,3,2,1,0:T(8,128)(2,1)} %bitcast.13), calls=%async_computation.1 | async-start | bytes 1048576 | tf_op jit(solution)/shard_map/all_to_all | solution.py:74
  21.2 0.5 slice.155
  21.7 0.5 slice.156
  22.4 1.0 copy.63
  23.5 1.0 copy.64
  24.6 0.1 fusion.43
  24.9 0.3 copy.66
  25.3 0.4 pad_maximum_fusion.3
  25.7 0.8 slice.154
  26.5 0.8 slice.153
  27.5 1.1 pad_maximum_fusion.2
  28.5 12.0 %all-to-all-done.1 = bf16[16,2,4,16,128]{4,3,2,1,0:T(8,128)(2,1)S(1)} async-done(((bf16[16,2,4,16,128]{4,3,2,1,0:T(8,128)(2,1)}), bf16[16,2,4,16,128]{4,3,2,1,0:T(8,128)(2,1)S(1)}, u32[]{:S(2)}, u32[]{:S(2)}) %all-to-all-start.1) | async-done | bytes 524320 | tf_op jit(solution)/shard_map/all_to_all | solution.py:74
  40.6 4.3 %all-to-all-start = ((bf16[16,2,7,16,128]{4,3,2,1,0:T(8,128)(2,1)}), bf16[16,2,7,16,128]{4,3,2,1,0:T(8,128)(2,1)}, u32[]{:S(2)}, u32[]{:S(2)}) async-start(bf16[16,2,7,16,128]{4,3,2,1,0:T(8,128)(2,1)} %bitcast.8), calls=%async_computation | async-start | bytes 1835008 | tf_op jit(solution)/shard_map/all_to_all | solution.py:116
  46.3 0.5 mul.430
  46.8 3.7 %mul.431 = bf16[3,256,256]{2,1,0:T(8,128)(2,1)} reshape(bf16[3,16,16,16,16]{4,3,2,1,0:T(8,128)(2,1)S(1)} %mul.430) | data formatting | bytes 786432 | tf_op jit(solution)/shard_map/mul | solution.py:39
  50.5 0.3 slice_reduce_fusion.4
  50.9 0.2 multiply_add_fusion
  51.2 1.1 bitcast_convert_fusion
  52.3 1.3 copy.74
  53.7 18.3 %all-to-all-done = bf16[16,2,7,16,128]{4,3,2,1,0:T(8,128)(2,1)} async-done(((bf16[16,2,7,16,128]{4,3,2,1,0:T(8,128)(2,1)}), bf16[16,2,7,16,128]{4,3,2,1,0:T(8,128)(2,1)}, u32[]{:S(2)}, u32[]{:S(2)}) %all-to-all-start) | async-done | bytes 917536 | tf_op jit(solution)/shard_map/all_to_all | solution.py:116
  72.0 1.4 copy.68
  73.6 0.3 copy.97
  74.1 1.2 fusion.62
  75.4 1.5 %broadcast_multiply_fusion = f32[16,16,16,16]{3,2,1,0:T(8,128)} fusion(f32[16,16]{1,0:T(8,128)S(1)} %fusion.50, f32[16,16,16]{2,1,0:T(8,128)S(1)} %bitcast.153), kind=kLoop, calls=%fused_computation.43 | loop fusion | flops 65536 | bytes 279552 | tf_op jit(solution)/shard_map/mul | solution.py:127
  76.9 2.4 %reshape.116 = f32[256,256,1,1]{1,0,2,3:T(8,128)S(1)} reshape(f32[16,16,16,16]{3,2,1,0:T(8,128)} %broadcast_multiply_fusion) | data formatting | bytes 524288 | tf_op jit(solution)/shard_map/mul | solution.py:127
  79.4 1.6 %fusion.31 = f32[2,4,256,128]{2,3,1,0:T(8,128)S(1)} fusion(f32[2,6,256,128]{2,3,1,0:T(8,128)S(1)} %convert_element_type.128, f32[2,4,256,1]{2,3,1,0:T(1,128)S(1)} %broadcast_in_dim.24, f32[2,4,256,127]{2,3,1,0:T(8,128)} %get-tuple-element.30, f32[2,4,256,127]{2,3,1,0:T(8,128)S(1)} %get-tuple-element.29, f32[2,4,256,1]{2,3,1,0:T(1,128)S(1)} %copy.73), kind=kLoop, calls=%fused_computation.41 | loop fusion | flops 1835008 | bytes 6291456 | tf_op jit(solution)/shard_map/sub | solution.py:30
  81.1 0.9 fusion.16
  82.0 1.1 fusion.65
  83.1 2.6 %collective-permute-start.5 = (f32[2,4,256]{2,1,0:T(4,128)S(1)}, f32[2,4,256]{2,1,0:T(4,128)S(1)}, u32[]{:S(2)}, u32[]{:S(2)}) collective-permute-start(f32[2,4,256]{2,1,0:T(4,128)S(1)} %bitcast.161), channel_id=1, source_target_pairs={{0,1},{1,2},{2,3},{4,5},{5,6},{6,7},{8,9},{9,10},{10,11},{12,13},{... | collective-permute-start | bytes 24584 | tf_op jit(solution)/shard_map/ppermute | solution.py:133
  85.8 1.3 collective-permute-start.4
  87.1 3.7 %collective-permute-start.3 = (f32[2,1,256,128]{2,3,1,0:T(8,128)S(1)}, f32[2,1,256,128]{2,3,1,0:T(8,128)S(1)}, u32[]{:S(2)}, u32[]{:S(2)}) collective-permute-start(f32[2,1,256,128]{2,3,1,0:T(8,128)S(1)} %get-tuple-element.25), channel_id=1, source_target_pairs={{0,4},{1,5},{2,6},{3,7},{4,8},{5,9},{6,10},{7,11},{8,12},{9,13},{1... | collective-permute-start | bytes 786440 | tf_op jit(solution)/shard_map/ppermute | solution.py:131
  90.7 5.1 %collective-permute-start.2 = (f32[2,1,256,128]{2,3,1,0:T(8,128)S(1)}, f32[2,1,256,128]{2,3,1,0:T(8,128)S(1)}, u32[]{:S(2)}, u32[]{:S(2)}) collective-permute-start(f32[2,1,256,128]{2,3,1,0:T(8,128)S(1)} %get-tuple-element.26), channel_id=1, source_target_pairs={{4,0},{5,1},{6,2},{7,3},{8,4},{9,5},{10,6},{11,7},{12,8},{13,9},{1... | collective-permute-start | bytes 786440 | tf_op jit(solution)/shard_map/ppermute | solution.py:132
  95.8 0.2 fusion.58
  96.1 5.8 %collective-permute-done.3 = f32[2,1,256,128]{2,3,1,0:T(8,128)S(1)} collective-permute-done((f32[2,1,256,128]{2,3,1,0:T(8,128)S(1)}, f32[2,1,256,128]{2,3,1,0:T(8,128)S(1)}, u32[]{:S(2)}, u32[]{:S(2)}) %collective-permute-start.3) | collective-permute-done | bytes 262176 | tf_op jit(solution)/shard_map/ppermute | solution.py:131
  101.9 5.3 %collective-permute-done.2 = f32[2,1,256,128]{2,3,1,0:T(8,128)S(1)} collective-permute-done((f32[2,1,256,128]{2,3,1,0:T(8,128)S(1)}, f32[2,1,256,128]{2,3,1,0:T(8,128)S(1)}, u32[]{:S(2)}, u32[]{:S(2)}) %collective-permute-start.2) | collective-permute-done | bytes 262176 | tf_op jit(solution)/shard_map/ppermute | solution.py:132
  107.4 0.2 fusion.61
  107.7 0.3 fusion.23
  107.9 1.1 fusion.21
  109.0 1.0 fusion.9
  110.1 0.3 copy.89
  110.5 37.4 %all_to_all.29 = f32[2,4,16,16,128]{4,3,1,0,2:T(8,128)S(1)} all-to-all(f32[2,4,16,16,128]{4,3,1,0,2:T(8,128)S(1)} %copy.90), channel_id=1, replica_groups=mesh['space'=32,'modes'=16] {'modes'}, dimensions={2} | all-to-all | bytes 2097152 | tf_op jit(solution)/shard_map/all_to_all | solution.py:156
  147.9 0.7 copy.91
  148.6 1.4 reshape.108
  (82 shorter events, 3.2 us)
Async XLA Ops:
  1.1 24.1 %collective-permute-start = (bf16[2,1,16,512]{3,1,2,0:T(2,128)(2,1)S(1)}, bf16[2,1,16,512]{3,1,2,0:T(2,128)(2,1)S(1)}, u32[]{:S(2)}, u32[]{:S(2)}) collective-permute-start(bf16[2,1,16,512]{3,1,2,0:T(2,128)(2,1)S(1)} %get-tuple-element.31), channel_id=1, source_target_pairs={{0,16},{16,32},{32,48},{48,64},{64,80},{80,96},{96,112},{112,128},... | collective-permute-start | bytes 98312 | tf_op jit(solution)/shard_map/ppermute | solution.py:14
  3.1 18.1 %copy-start.5 = (f32[1,16,16]{2,1,0:T(8,128)S(1)}, f32[1,16,16]{2,1,0:T(8,128)}, u32[]{:S(2)}) copy-start(f32[1,16,16]{2,1,0:T(8,128)} %param.15) | copy-start | bytes 3076
  3.1 18.1 %copy-start = (bf16[2,16,16,512]{3,2,1,0:T(8,128)(2,1)S(1)}, bf16[2,16,16,512]{3,2,1,0:T(8,128)(2,1)}, u32[]{:S(2)}) copy-start(bf16[2,16,16,512]{3,2,1,0:T(8,128)(2,1)} %param.9) | copy-start | bytes 1572868
  3.1 22.2 %collective-permute-start.1 = (bf16[2,1,16,512]{3,1,2,0:T(2,128)(2,1)S(1)}, bf16[2,1,16,512]{3,1,2,0:T(2,128)(2,1)S(1)}, u32[]{:S(2)}, u32[]{:S(2)}) collective-permute-start(bf16[2,1,16,512]{3,1,2,0:T(2,128)(2,1)S(1)} %get-tuple-element.32), channel_id=1, source_target_pairs={{16,0},{32,16},{48,32},{64,48},{80,64},{96,80},{112,96},{128,112},... | collective-permute-start | bytes 98312 | tf_op jit(solution)/shard_map/ppermute | solution.py:15
  9.2 31.4 %all-to-all-start.1 = ((bf16[16,2,4,16,128]{4,3,2,1,0:T(8,128)(2,1)}), bf16[16,2,4,16,128]{4,3,2,1,0:T(8,128)(2,1)S(1)}, u32[]{:S(2)}, u32[]{:S(2)}) async-start(bf16[16,2,4,16,128]{4,3,2,1,0:T(8,128)(2,1)} %bitcast.13), calls=%async_computation.1 | async-start | bytes 1048576 | tf_op jit(solution)/shard_map/all_to_all | solution.py:74
  27.5 17.5 %copy-start.4 = (f32[2,3,8]{2,0,1:T(2,128)S(1)}, f32[2,3,8]{2,0,1:T(2,128)}, u32[]{:S(2)}) copy-start(f32[2,3,8]{2,0,1:T(2,128)} %param.12) | copy-start | bytes 580
  27.5 17.6 %copy-start.8 = (s32[3,16,16]{2,1,0:T(8,128)S(1)}, s32[3,16,16]{2,1,0:T(8,128)}, u32[]{:S(2)}) copy-start(s32[3,16,16]{2,1,0:T(8,128)} %param.14) | copy-start | bytes 9220
  27.5 18.4 %copy-start.7 = (s32[16,512]{1,0:T(8,128)S(1)}, s32[16,512]{1,0:T(8,128)}, u32[]{:S(2)}) copy-start(s32[16,512]{1,0:T(8,128)} %param.10) | copy-start | bytes 98308
  40.6 5.6 %copy-start.1 = (bf16[16,2,4,16,128]{4,3,2,1,0:T(8,128)(2,1)}, bf16[16,2,4,16,128]{4,3,2,1,0:T(8,128)(2,1)S(1)}, u32[]{:S(2)}) copy-start(bf16[16,2,4,16,128]{4,3,2,1,0:T(8,128)(2,1)S(1)} %all-to-all-done.1) | copy-start | bytes 1572868
  40.6 31.4 %all-to-all-start = ((bf16[16,2,7,16,128]{4,3,2,1,0:T(8,128)(2,1)}), bf16[16,2,7,16,128]{4,3,2,1,0:T(8,128)(2,1)}, u32[]{:S(2)}, u32[]{:S(2)}) async-start(bf16[16,2,7,16,128]{4,3,2,1,0:T(8,128)(2,1)} %bitcast.8), calls=%async_computation | async-start | bytes 1835008 | tf_op jit(solution)/shard_map/all_to_all | solution.py:116
  46.7 3.7 %copy-start.6 = (f32[2,8]{1,0:T(2,128)S(1)}, f32[2,8]{1,0:T(2,128)}, u32[]{:S(2)}) copy-start(f32[2,8]{1,0:T(2,128)} %param.11) | copy-start | bytes 196
  79.4 1.7 %copy-start.2 = (f32[2,4,256,128]{2,3,1,0:T(8,128)S(1)}, f32[2,4,256,128]{2,3,1,0:T(8,128)}, u32[]{:S(2)}) copy-start(f32[2,4,256,128]{2,3,1,0:T(8,128)} %copy.74) | copy-start | bytes 3145732
  79.4 1.7 %copy-start.3 = (bf16[3,256,256]{2,1,0:T(8,128)(2,1)S(1)}, bf16[3,256,256]{2,1,0:T(8,128)(2,1)}, u32[]{:S(2)}) copy-start(bf16[3,256,256]{2,1,0:T(8,128)(2,1)} %mul.431) | copy-start | bytes 1179652
  79.4 1.7 %copy-start.9 = (bf16[3,256,256]{2,1,0:T(8,128)(2,1)S(1)}, bf16[3,256,256]{2,1,0:T(8,128)(2,1)}, u32[]{:S(2)}) copy-start(bf16[3,256,256]{2,1,0:T(8,128)(2,1)} %param.13) | copy-start | bytes 1179652
  83.1 12.9 %collective-permute-start.5 = (f32[2,4,256]{2,1,0:T(4,128)S(1)}, f32[2,4,256]{2,1,0:T(4,128)S(1)}, u32[]{:S(2)}, u32[]{:S(2)}) collective-permute-start(f32[2,4,256]{2,1,0:T(4,128)S(1)} %bitcast.161), channel_id=1, source_target_pairs={{0,1},{1,2},{2,3},{4,5},{5,6},{6,7},{8,9},{9,10},{10,11},{12,13},{... | collective-permute-start | bytes 24584 | tf_op jit(solution)/shard_map/ppermute | solution.py:133
  85.8 10.3 %collective-permute-start.4 = (f32[2,4,256]{2,1,0:T(4,128)S(1)}, f32[2,4,256]{2,1,0:T(4,128)S(1)}, u32[]{:S(2)}, u32[]{:S(2)}) collective-permute-start(f32[2,4,256]{2,1,0:T(4,128)S(1)} %bitcast.160), channel_id=1, source_target_pairs={{1,0},{2,1},{3,2},{5,4},{6,5},{7,6},{9,8},{10,9},{11,10},{13,12},{... | collective-permute-start | bytes 24584 | tf_op jit(solution)/shard_map/ppermute | solution.py:134
  87.1 14.8 %collective-permute-start.3 = (f32[2,1,256,128]{2,3,1,0:T(8,128)S(1)}, f32[2,1,256,128]{2,3,1,0:T(8,128)S(1)}, u32[]{:S(2)}, u32[]{:S(2)}) collective-permute-start(f32[2,1,256,128]{2,3,1,0:T(8,128)S(1)} %get-tuple-element.25), channel_id=1, source_target_pairs={{0,4},{1,5},{2,6},{3,7},{4,8},{5,9},{6,10},{7,11},{8,12},{9,13},{1... | collective-permute-start | bytes 786440 | tf_op jit(solution)/shard_map/ppermute | solution.py:131
  90.7 16.4 %collective-permute-start.2 = (f32[2,1,256,128]{2,3,1,0:T(8,128)S(1)}, f32[2,1,256,128]{2,3,1,0:T(8,128)S(1)}, u32[]{:S(2)}, u32[]{:S(2)}) collective-permute-start(f32[2,1,256,128]{2,3,1,0:T(8,128)S(1)} %get-tuple-element.26), channel_id=1, source_target_pairs={{4,0},{5,1},{6,2},{7,3},{8,4},{9,5},{10,6},{11,7},{12,8},{13,9},{1... | collective-permute-start | bytes 786440 | tf_op jit(solution)/shard_map/ppermute | solution.py:132
